TPU v7x, 256 devices: a whole 4x4x8 slice. The times are simulated.
256 devices in a mesh: facet: 8 (over y_lo, x), vis: 16 (over z, core), spec: 2 (over y_hi).
Axes of the slice: x: 4, y: 4 (y_hi: 2, y_lo: 2; y = y_hi * 2 + y_lo), z: 8, core: 2. Of those that a mesh axis runs over, the one named last changes fastest.
Arguments:
- image: float32 [1024, 8, 4096], P(('facet', 'vis'), 'spec'), may hold values from 0 to 1
- wavelet_dual: float32 [1024, 8, 4096], P(('facet', 'vis'), 'spec'), may hold values from -6 to 6
- weights: float32 [1024, 4096], P(('facet', 'vis')), may hold values from 0.3 to 3
- kernels: bfloat16 [8, 16, 2, 256, 128], P('facet', 'vis'), may hold values from -0.375 to 0.375
- vis_data: bfloat16 [8, 16, 8, 2, 16, 256, 128], P('facet', 'vis', 'spec'), may hold values from -6 to 6
- tile_list: int32 [8, 16, 16], P('facet', 'vis'), may hold values from 0 to 31, as said below
- tile_count: int32 [8, 16], P('facet', 'vis'), may hold values from 4 to 16, as said below
Outputs:
- image_next: float32 [1024, 8, 4096], P(('facet', 'vis'), 'spec')
- dual_next: float32 [1024, 8, 4096], P(('facet', 'vis'), 'spec')
Inputs may be any that keep to these rules, and one draw needn't show every extreme that they name: `tile_list`: the 16 slots of a block name distinct tiles; slots from tile_count on are unused. `tile_count`: every draw has a block with 16 occupied slots and one with the fewest allowed.
All inputs are finite; a program needn't handle non-finite values.
Results may differ from a plain program's by a relative error of at most 0.017.
Values may be sent and summed in bfloat16 or wider, within the bound.
No kernel may reach another device: no remote copies, remote signals or barrier semaphores. Data moves between devices by JAX's collectives and lax.ppermute only.
A program may use at most 128 MiB of HBM per device.

v0:
```python
import math

import jax
import jax.numpy as jnp
from jax import lax
from jax.sharding import PartitionSpec as P

root_three = math.sqrt(3.0)
norm_factor = 4.0 * math.sqrt(2.0)
low_taps = [
    (1.0 + root_three) / norm_factor,
    (3.0 + root_three) / norm_factor,
    (3.0 - root_three) / norm_factor,
    (1.0 - root_three) / norm_factor,
]
high_taps = [low_taps[3], -low_taps[2], low_taps[1], -low_taps[0]]
primal_step = 0.2
dual_step = 0.5
tile_width = 128
highest = lax.Precision.HIGHEST


def shifted(value, axis, steps):
    count = lax.axis_size(axis)
    initial, last = (max(0, -steps), min(count, count - steps))
    return lax.ppermute(value, axis, [(source, source + steps) for source in range(initial, last)])


def for_sending(x):

    def short(part):
        return part.astype(jnp.bfloat16) if part.dtype == jnp.float32 else part

    return jax.tree.map(short, x)


def phase_table(rows_count, cols_count, modulus):
    rows_index = jnp.arange(rows_count, dtype=jnp.int32)
    cols_index = jnp.arange(cols_count, dtype=jnp.int32)
    angle = (rows_index[:, None] * cols_index[None, :] % modulus).astype(jnp.float32) * (
        2.0 * math.pi / modulus
    )
    return (jnp.cos(angle), jnp.sin(angle))


def across_outer(values, table):
    return jnp.einsum(
        "qab,ak->qkb", values, table, precision=highest, preferred_element_type=jnp.float32
    )


def along_inner(values, table):
    return jnp.einsum(
        "qkb,bj->qkj", values, table, precision=highest, preferred_element_type=jnp.float32
    )


def fourier_rows(real_part, imag_part, sign):
    rows_count, length = real_part.shape
    outer = length // tile_width
    cos_outer, sin_outer = phase_table(outer, outer, outer)
    cos_twist, sin_twist = phase_table(outer, tile_width, length)
    cos_inner, sin_inner = phase_table(tile_width, tile_width, tile_width)
    first_re = real_part.reshape(rows_count, outer, tile_width)
    first_im = imag_part.reshape(rows_count, outer, tile_width)
    section_re = across_outer(first_re, cos_outer) - sign * across_outer(first_im, sin_outer)
    section_im = across_outer(first_im, cos_outer) + sign * across_outer(first_re, sin_outer)
    twist_re = section_re * cos_twist - sign * section_im * sin_twist
    twist_im = section_im * cos_twist + sign * section_re * sin_twist
    final_re = along_inner(twist_re, cos_inner) - sign * along_inner(twist_im, sin_inner)
    final_im = along_inner(twist_im, cos_inner) + sign * along_inner(twist_re, sin_inner)
    unit_scale = 1.0 / math.sqrt(length)
    final_re = jnp.swapaxes(final_re, 1, 2).reshape(rows_count, length) * unit_scale
    final_im = jnp.swapaxes(final_im, 1, 2).reshape(rows_count, length) * unit_scale
    return (final_re, final_im)


def kernel_blocks(kernel_pair):
    real_k = kernel_pair[0]
    imag_k = kernel_pair[1]
    top_row = jnp.stack([real_k, -imag_k], axis=1)
    bottom_row = jnp.stack([imag_k, real_k], axis=1)
    return jnp.stack([top_row, bottom_row], axis=0)


def angle_table(first, second, modulus):
    angle = ((first[:, None] * second[None, :]) % modulus).astype(jnp.float32) * (
        2.0 * math.pi / modulus
    )
    return (jnp.cos(angle), jnp.sin(angle))


def precise(spec, left, right):
    return jnp.einsum(
        spec, left, right, precision=lax.Precision.HIGH, preferred_element_type=jnp.float32
    )


def split_table(spec, values, table):
    high = table.astype(jnp.bfloat16)
    low = (table - high.astype(jnp.float32)).astype(jnp.bfloat16)
    return jnp.einsum(spec, values, high, preferred_element_type=jnp.float32) + jnp.einsum(
        spec, values, low, preferred_element_type=jnp.float32
    )


def per_device(image, wavelet_dual, weights, kernels, vis_data, tile_list, tile_count):
    panel_rows, chan_count, grid_width = image.shape
    inner = tile_width
    outer = grid_width // inner
    unit_scale = 1.0 / math.sqrt(grid_width)
    bf = jnp.bfloat16
    f32 = jnp.float32
    own_list = tile_list[0, 0]
    own_count = tile_count[0, 0]
    slots_count = own_list.shape[0]
    image_rows = image.reshape(panel_rows * chan_count, grid_width)
    grid_re, grid_im = fourier_rows(image_rows, jnp.zeros_like(image_rows), -1.0)
    grid_panel = (
        jnp.stack([grid_re, grid_im], axis=1)
        .reshape(panel_rows, chan_count, 2, grid_width)
        .astype(bf)
    )
    gathered = lax.all_gather(grid_panel, "vis", axis=0, tiled=True)
    facet_rows = gathered.shape[0]
    split_rows = gathered.reshape(facet_rows, chan_count, 2, outer, inner)
    tiles = jnp.take(split_rows, own_list, axis=3)
    stacked = kernel_blocks(kernels[0, 0])
    predicted = jnp.einsum(
        "omir,rcisn->cosmn", stacked, tiles, preferred_element_type=f32
    )
    own_data = vis_data[0, 0]
    live_slots = (jnp.arange(slots_count, dtype=jnp.int32) < own_count)[None, None, :, None, None]
    residual = jnp.where(live_slots, predicted - own_data.astype(f32), 0.0).astype(bf)
    blocks = facet_rows // panel_rows
    stacked5 = stacked.reshape(2, -1, 2, blocks, panel_rows)
    partial = jnp.einsum(
        "omivr,cosmn->iscvrn", stacked5, residual, preferred_element_type=f32
    ).astype(bf)
    inner_index = jnp.arange(inner, dtype=jnp.int32)
    outer_index = jnp.arange(outer, dtype=jnp.int32)
    cos_in, sin_in = angle_table(inner_index, inner_index, inner)
    cos_tw, sin_tw = angle_table(outer_index, inner_index, grid_width)
    cos_sel, sin_sel = angle_table(outer_index, own_list, outer)
    tw_c = cos_tw[None, :, None, None, :]
    tw_s = sin_tw[None, :, None, None, :]
    inv_c = jnp.transpose(cos_sel).astype(bf)
    inv_s = jnp.transpose(sin_sel).astype(bf)
    back_re = jnp.einsum("sa,scvrk->vacrk", inv_c, partial[0], preferred_element_type=f32) - jnp.einsum(
        "sa,scvrk->vacrk", inv_s, partial[1], preferred_element_type=f32
    )
    back_im = jnp.einsum("sa,scvrk->vacrk", inv_s, partial[0], preferred_element_type=f32) + jnp.einsum(
        "sa,scvrk->vacrk", inv_c, partial[1], preferred_element_type=f32
    )
    turned_re = (back_re * tw_c - back_im * tw_s).astype(bf)
    turned_im = (back_re * tw_s + back_im * tw_c).astype(bf)
    out_c = (cos_in * unit_scale).astype(bf)
    out_s = (sin_in * unit_scale).astype(bf)
    rows_part = jnp.einsum("vacrk,kb->vacrb", turned_re, out_c, preferred_element_type=f32) - jnp.einsum(
        "vacrk,kb->vacrb", turned_im, out_s, preferred_element_type=f32
    )
    rows_sum = lax.psum_scatter(rows_part.astype(bf), "vis", scatter_dimension=0, tiled=True)
    gradient = (
        jnp.transpose(rows_sum[0].astype(f32), (2, 1, 3, 0))
        .reshape(panel_rows, chan_count, grid_width)
    )
    upper_rim = shifted(
        wavelet_dual[panel_rows - 3 :].astype(jnp.bfloat16), ("facet", "vis"), 1
    ).astype(jnp.float32)
    padded_dual = jnp.concatenate([upper_rim, wavelet_dual], axis=0)
    synthesized = jnp.zeros_like(wavelet_dual)
    for offset in range(4):
        synthesized = (
            synthesized + high_taps[offset] * padded_dual[3 - offset : 3 - offset + panel_rows]
        )
    image_next = jnp.maximum(image - primal_step * (gradient + synthesized), 0.0)
    extrap = 2.0 * image_next - image
    lower_rim = shifted(for_sending(extrap[:3]), ("facet", "vis"), -1)
    padded_next = jnp.concatenate([extrap, lower_rim], axis=0)
    detail = jnp.zeros_like(extrap)
    for offset in range(4):
        detail = detail + high_taps[offset] * padded_next[offset : offset + panel_rows]
    update = wavelet_dual + dual_step * detail
    own_energy = jnp.sum(update * update, axis=1)
    other_energy = lax.ppermute(own_energy.astype(bf), "spec", [(0, 1), (1, 0)])
    energy = own_energy + other_energy.astype(f32)
    dual_next = update * weights[:, None, :] / jnp.maximum(weights, jnp.sqrt(energy))[:, None, :]
    return (image_next, dual_next)


def solution(mesh):
    return jax.shard_map(
        per_device,
        mesh=mesh,
        in_specs=(
            P(("facet", "vis"), "spec", None),
            P(("facet", "vis"), "spec", None),
            P(("facet", "vis"), None),
            P("facet", "vis", None, None, None),
            P("facet", "vis", "spec", None, None, None, None),
            P("facet", "vis", None),
            P("facet", "vis"),
        ),
        out_specs=(P(("facet", "vis"), "spec", None), P(("facet", "vis"), "spec", None)),
        check_vma=False,
    )
```

profile of v0, /device:TPU:24, one launch (start us, length us, event | category | flops | bytes accessed | tf_op | source)
XLA Modules:
  0.0 248.5 jit_solution(831710101602006696)
XLA Ops:
  7.7 1.4 reshape_reshape.3
  18.5 1.2 pad_maximum_fusion.2
  19.9 11.5 %copy.57 = bf16[1,1,4,2,16,256,128]{5,6,4,3,2,1,0:T(8,128)(2,1)} copy(bf16[1,1,4,2,16,256,128]{6,5,4,3,2,1,0:T(8,128)(2,1)} %param.11) | data formatting | bytes 16777216 | tf_op args[4]
  32.6 45.9 %all-gather.2.cloned.1.call-done = bf16[128,4,2,4096]{3,1,0,2:T(4,128)(2,1)} async-done(((bf16[8,4,2,4096]{3,1,0,2:T(4,128)(2,1)}), bf16[128,4,2,4096]{3,1,0,2:T(4,128)(2,1)}) %all-gather.2.cloned.1.call-update) | async-done | bytes 8388624 | tf_op jit(solution)/shard_map/all_gather | solution.py:124
  78.4 14.5 %copy.54 = bf16[128,4,2,4096]{0,3,2,1:T(8,128)(2,1)} copy(bf16[128,4,2,4096]{3,1,0,2:T(4,128)(2,1)} %all-gather.2.cloned.1.call-done) | data formatting | bytes 16777216 | tf_op jit(solution)/shard_map/all_gather | solution.py:124
  93.0 12.0 %copy.55 = bf16[128,4,2,32,128]{4,0,3,2,1:T(8,128)(2,1)} copy(bf16[128,4,2,32,128]{0,4,3,2,1:T(8,128)(2,1)} %bitcast.144) | data formatting | bytes 16777216 | tf_op jit(solution)/shard_map/reshape | solution.py:126
  105.0 6.4 %gather_fusion = bf16[16,128,4,2,128]{4,1,3,2,0:T(8,128)(2,1)} fusion(bf16[128,4,2,32,128]{4,0,3,2,1:T(8,128)(2,1)} %copy.55, s32[1024]{0:T(1024)S(1)} %pad_clamp_fusion), kind=kCustom, calls=%fused_computation | custom fusion | bytes 8388672 | tf_op jit(solution)/shard_map/jit(_take)/gather | solution.py:127
  111.4 9.2 %fusion.8 = bf16[4,2,16,256,128,1,1]{3,4,2,1,0,6,5:T(8,128)(2,1)S(1)} fusion(bf16[1,1,4,2,16,256,128]{5,6,4,3,2,1,0:T(8,128)(2,1)} %copy.57, pred[16]{0:T(512)(128)(4,1)S(1)} %iota_compare_fusion, bf16[1,256,2,128]{3,1,2,0:T(8,128)(2,1)S(1)} %get-tuple-element.23, bf16[1,256,2,128]{3,1,2,0:T(8,128)(2,1)S(1)} %get-tuple-element.22, ...), kind=kOutput, calls=%fused_computation.16 | convolution fusion | flops 2166882304 | bytes 21233696 | tf_op jit(solution)/shard_map/omir,rcisn->cosmn/dot_general | solution.py:129
  120.6 2.7 %fusion.9 = bf16[2,16,4,16,8,128]{5,3,4,0,1,2:T(8,128)(2,1)S(1)} fusion(bf16[4,2,16,256,128,1,1]{3,4,2,1,0,6,5:T(8,128)(2,1)S(1)} %fusion.8, bf16[1,256,1,16,8]{1,3,0,4,2:T(8,128)(2,1)S(1)} %copy.61, bf16[1,256,1,16,8]{1,3,0,4,2:T(8,128)(2,1)S(1)} %get-tuple-element.21, bf16[1,256,1,16,8]{1,3,0,4,2:T(8,128)(2,1)S(1)} %get-tuple-element.20), kind=kOutput, calls=%fused_computation.17 | convolution fusion | flops 2150629376 | bytes 12779520 | tf_op jit(solution)/shard_map/omivr,cosmn->iscvrn/dot_general | solution.py:137
  124.4 1.8 fusion.19
  126.1 5.0 %fusion.21 = f32[4,16,8,128,32]{3,4,2,1,0:T(8,128)} fusion(bf16[16,4,16,8,128]{4,2,3,0,1:T(8,128)(2,1)S(1)} %get-tuple-element.12, s32[16]{0:T(128)S(1)} %bitcast.148), kind=kOutput, calls=%fused_computation.28 | convolution fusion | flops 67116544 | bytes 10485824 | tf_op jit(solution)/shard_map/sa,scvrk->vacrk/dot_general | solution.py:149
  131.2 5.0 %fusion.25 = f32[4,16,8,128,32]{3,4,2,1,0:T(8,128)} fusion(bf16[16,4,16,8,128]{4,2,3,0,1:T(8,128)(2,1)S(1)} %get-tuple-element.13, s32[16]{0:T(128)S(1)} %bitcast.149), kind=kOutput, calls=%fused_computation.32 | convolution fusion | flops 67116544 | bytes 10485824 | tf_op jit(solution)/shard_map/sa,scvrk->vacrk/dot_general | solution.py:149
  136.2 15.4 %fusion.3 = (bf16[16,32,4,8,128]{4,1,3,0,2:T(8,128)(2,1)}, bf16[16,32,4,8,128]{4,1,3,0,2:T(8,128)(2,1)}) fusion(f32[32,128]{1,0:T(8,128)S(1)} %fusion.122, f32[32,128]{1,0:T(8,128)S(1)} %get-tuple-element.25, f32[4,16,8,128,32]{3,4,2,1,0:T(8,128)S(1)} %fusion.19, f32[4,16,8,128,32]{3,4,2,1,0:T(8,128)} %fusion.25, f32[4,16,8,128,32]{3,4,2,1,0:T(8,128)} %fusion.21, ...), kind=kOutput, calls=%fused_computation.7 | convolution fusion | flops 88088064 | bytes 35684416 | tf_op jit(solution)/shard_map/sa,scvrk->vacrk/dot_general | solution.py:152
  151.6 4.4 %fusion.11 = f32[16,32,4,8,128]{4,3,2,1,0:T(8,128)S(1)} fusion(bf16[16,32,4,8,128]{4,1,3,0,2:T(8,128)(2,1)} %get-tuple-element.11), kind=kOutput, calls=%fused_computation.19 | convolution fusion | flops 537133056 | bytes 12582912 | tf_op jit(solution)/shard_map/vacrk,kb->vacrb/dot_general | solution.py:159
  156.0 4.2 %subtract_convert_fusion = bf16[16,32,4,8,128]{4,3,2,1,0:T(8,128)(2,1)} fusion(f32[16,32,4,8,128]{4,3,2,1,0:T(8,128)S(1)} %fusion.11, bf16[16,32,4,8,128]{4,1,3,0,2:T(8,128)(2,1)S(1)} %copy-done.1), kind=kOutput, calls=%fused_computation.15 | convolution fusion | flops 541327360 | bytes 16777216 | tf_op jit(solution)/shard_map/vacrk,kb->vacrb/dot_general | solution.py:159
  161.6 2.2 collective-permute-start
  163.8 8.3 %collective-permute-done = bf16[3,4,4096]{2,0,1:T(4,128)(2,1)S(1)} collective-permute-done((bf16[3,4,4096]{2,0,1:T(4,128)(2,1)S(1)}, bf16[3,4,4096]{2,0,1:T(4,128)(2,1)S(1)}, u32[]{:S(2)}, u32[]{:S(2)}) %collective-permute-start) | collective-permute-done | bytes 98336 | tf_op jit(solution)/shard_map/ppermute | solution.py:26
  172.1 49.5 %reduce-scatter.2.cloned.1.call-done = bf16[1,32,4,8,128]{4,3,2,1,0:T(8,128)(2,1)} async-done(((bf16[16,32,4,8,128]{4,3,2,1,0:T(8,128)(2,1)}), bf16[1,32,4,8,128]{4,3,2,1,0:T(8,128)(2,1)}) %reduce-scatter.2.cloned.1.call-update) | async-done | bytes 262160 | tf_op jit(solution)/shard_map/reduce_scatter | solution.py:162
  224.2 1.7 multiply_subtract_fusion
  226.0 4.4 %collective-permute-start.1 = (bf16[3,4,4096]{2,0,1:T(4,128)(2,1)S(1)}, bf16[3,4,4096]{2,0,1:T(4,128)(2,1)S(1)}, u32[]{:S(2)}, u32[]{:S(2)}) collective-permute-start(bf16[3,4,4096]{2,0,1:T(4,128)(2,1)S(1)} %slice.135), channel_id=1, source_target_pairs={{2,0},{4,2},{6,4},{8,6},{10,8},{12,10},{14,12},{16,14},{18,16},{20... | collective-permute-start | bytes 294920 | tf_op jit(solution)/shard_map/ppermute | solution.py:26
  230.3 2.5 %collective-permute-done.1 = bf16[3,4,4096]{2,0,1:T(4,128)(2,1)S(1)} collective-permute-done((bf16[3,4,4096]{2,0,1:T(4,128)(2,1)S(1)}, bf16[3,4,4096]{2,0,1:T(4,128)(2,1)S(1)}, u32[]{:S(2)}, u32[]{:S(2)}) %collective-permute-start.1) | collective-permute-done | bytes 98336 | tf_op jit(solution)/shard_map/ppermute | solution.py:26
  232.9 1.7 multiply_reduce_fusion
  234.6 1.3 collective-permute-start.2
  237.0 3.4 %collective-permute-done.2 = bf16[8,4096]{1,0:T(8,128)(2,1)S(1)} collective-permute-done((bf16[8,4096]{1,0:T(8,128)(2,1)S(1)}, bf16[8,4096]{1,0:T(8,128)(2,1)S(1)}, u32[]{:S(2)}, u32[]{:S(2)}) %collective-permute-start.2) | collective-permute-done | bytes 65568 | tf_op jit(solution)/shard_map/ppermute | solution.py:185
  (55 shorter events, 18.0 us)
Async XLA Ops:
  7.2 71.3 %all-gather.2.cloned.1.call-start = ((), (), s32[]{:S(2)}) async-start(), calls=%async_computation.1 | async-start | bytes 8912896 | tf_op jit(solution)/shard_map/all_gather | solution.py:124
  19.7 12.4 %copy-start.4 = (bf16[1,1,2,256,128]{4,3,2,1,0:T(8,128)(2,1)S(1)}, bf16[1,1,2,256,128]{4,3,2,1,0:T(8,128)(2,1)}, u32[]{:S(2)}) copy-start(bf16[1,1,2,256,128]{4,3,2,1,0:T(8,128)(2,1)} %param.10) | copy-start | bytes 393220
  19.7 12.7 %copy-start.5 = (s32[1,1,16]{2,1,0:T(1,128)S(1)}, s32[1,1,16]{2,1,0:T(1,128)}, u32[]{:S(2)}) copy-start(s32[1,1,16]{2,1,0:T(1,128)} %param.12) | copy-start | bytes 196
  19.7 201.9 %reduce-scatter.2.cloned.1.call-start = ((), (), s32[]{:S(2)}) async-start(), calls=%async_computation.2 | async-start | bytes 4456448 | tf_op jit(solution)/shard_map/reduce_scatter | solution.py:162
  124.3 6.8 %copy-start = (bf16[16,4,16,8,128]{4,2,3,0,1:T(8,128)(2,1)}, bf16[16,4,16,8,128]{4,2,3,0,1:T(8,128)(2,1)S(1)}, u32[]{:S(2)}) copy-start(bf16[16,4,16,8,128]{4,2,3,0,1:T(8,128)(2,1)S(1)} %get-tuple-element.13) | copy-start | bytes 6291460
  151.6 4.4 %copy-start.1 = (bf16[16,32,4,8,128]{4,1,3,0,2:T(8,128)(2,1)S(1)}, bf16[16,32,4,8,128]{4,1,3,0,2:T(8,128)(2,1)}, u32[]{:S(2)}) copy-start(bf16[16,32,4,8,128]{4,1,3,0,2:T(8,128)(2,1)} %get-tuple-element.10) | copy-start | bytes 12582916
  160.2 1.0 copy-start.2
  161.6 10.5 %collective-permute-start = (bf16[3,4,4096]{2,0,1:T(4,128)(2,1)S(1)}, bf16[3,4,4096]{2,0,1:T(4,128)(2,1)S(1)}, u32[]{:S(2)}, u32[]{:S(2)}) collective-permute-start(bf16[3,4,4096]{2,0,1:T(4,128)(2,1)S(1)} %slice.136), channel_id=1, source_target_pairs={{0,2},{2,4},{4,6},{6,8},{8,10},{10,12},{12,14},{14,16},{16,18},{18... | collective-permute-start | bytes 294920 | tf_op jit(solution)/shard_map/ppermute | solution.py:26
  223.3 17.1 %copy-start.3 = (f32[8,4096]{1,0:T(8,128)S(1)}, f32[8,4096]{1,0:T(8,128)}, u32[]{:S(2)}) copy-start(f32[8,4096]{1,0:T(8,128)} %param.9) | copy-start | bytes 393220
  226.0 6.9 %collective-permute-start.1 = (bf16[3,4,4096]{2,0,1:T(4,128)(2,1)S(1)}, bf16[3,4,4096]{2,0,1:T(4,128)(2,1)S(1)}, u32[]{:S(2)}, u32[]{:S(2)}) collective-permute-start(bf16[3,4,4096]{2,0,1:T(4,128)(2,1)S(1)} %slice.135), channel_id=1, source_target_pairs={{2,0},{4,2},{6,4},{8,6},{10,8},{12,10},{14,12},{16,14},{18,16},{20... | collective-permute-start | bytes 294920 | tf_op jit(solution)/shard_map/ppermute | solution.py:26
  234.6 5.9 %collective-permute-start.2 = (bf16[8,4096]{1,0:T(8,128)(2,1)S(1)}, bf16[8,4096]{1,0:T(8,128)(2,1)S(1)}, u32[]{:S(2)}, u32[]{:S(2)}) collective-permute-start(bf16[8,4096]{1,0:T(8,128)(2,1)S(1)} %convert_element_type.134), channel_id=1, source_target_pairs={{0,1},{1,0},{2,3},{3,2},{4,5},{5,4},{6,7},{7,6},{8,9},{9,8},{10,11... | collective-permute-start | bytes 196616 | tf_op jit(solution)/shard_map/ppermute | solution.py:185
Sparse Core Ops, SparseCore 0:
  19.8 58.5 all-gather.1
  160.3 61.2 reduce-scatter.1
where the time goes:
time: 250 us; the launch traced here: 249 us
  waiting for transfers between devices  110 us (44%)
  local copies, waits for them, and re-layouts  55.5 us (22%)
  matrix products  54.3 us (22%)
  between operations  15 us (6%)
  starting transfers between devices  8.14 us (3%)
  other arithmetic  5.92 us (2%)
    reduce_scatter x1, waiting for transfers between devices, per_device(): lax.psum_scatter(rows_part.astype(bf), 'vis', scatter_dimension=0, tiled=...  49.5 us
    all_gather x1, waiting for transfers between devices, per_device(): gathered = lax.all_gather(grid_panel, 'vis', axis=0, tiled=True)  45.9 us
    dot_general x1, matrix products, per_device(): jnp.einsum('sa,scvrk->vacrk', inv_s, partial[0], preferred_element_type=f32)  15.4 us
    unnamed x16, local copies, waits for them, and re-layouts  15.1 us
    all_gather x1, local copies, waits for them, and re-layouts, per_device(): gathered = lax.all_gather(grid_panel, 'vis', axis=0, tiled=True)  14.5 us
    reshape x1, local copies, waits for them, and re-layouts, per_device(): split_rows = gathered.reshape(facet_rows, chan_count, 2, outer, inner)  12 us
    ppermute x2, waiting for transfers between devices, shifted(): lax.ppermute(value, axis, [(source, source + steps) for source in range(i...  10.8 us
    dot_general x1, matrix products, per_device(): jnp.einsum('omir,rcisn->cosmn', stacked, tiles, preferred_element_type=f32)  9.22 us
  transfers between devices with their start and end apart: 5, of which 5 were waited for; matrix products, arithmetic and copies ran while one was open for 5% of the time, Pallas kernels for 0%

commit v1 on v0

--- a/solution.py
+++ b/solution.py
@@ -4,6 +4,8 @@
 import jax.numpy as jnp
 from jax import lax
 from jax.sharding import PartitionSpec as P
+from jax.experimental import pallas as pl
+from jax.experimental.pallas import tpu as pltpu
 
 root_three = math.sqrt(3.0)
 norm_factor = 4.0 * math.sqrt(2.0)
@@ -104,6 +106,56 @@
     )
 
 
+def degrid_body(list_ref, count_ref, kmat_ref, kadj_ref, grid_ref, vis_ref, out_ref):
+    slot = pl.program_id(1)
+
+    @pl.when(slot < count_ref[0])
+    def _():
+        rows = grid_ref.shape[0] * grid_ref.shape[1] * grid_ref.shape[2]
+        tile = grid_ref[...].astype(jnp.float32).reshape(rows, grid_ref.shape[3]).astype(jnp.bfloat16)
+        predicted = jnp.dot(kmat_ref[...], tile, preferred_element_type=jnp.float32)
+        measured = vis_ref[...].astype(jnp.float32).reshape(predicted.shape)
+        residual = (predicted - measured).astype(jnp.bfloat16)
+        gridded = jnp.dot(kadj_ref[...], residual, preferred_element_type=jnp.float32)
+        out_ref[...] = gridded.astype(out_ref.dtype)
+
+    @pl.when(slot >= count_ref[0])
+    def _():
+        out_ref[...] = jnp.zeros_like(out_ref)
+
+
+def degrid_grid(own_list, own_count, kernel_mat, kernel_adj, gathered, own_data):
+    blocks, chans, parts, rows, width = gathered.shape
+    slots = own_list.shape[0]
+    out_rows, in_rows = kernel_mat.shape
+    inner = tile_width
+    flops = 4 * out_rows * in_rows * inner * chans * slots
+    return pl.pallas_call(
+        degrid_body,
+        grid_spec=pltpu.PrefetchScalarGridSpec(
+            num_scalar_prefetch=2,
+            grid=(chans, slots),
+            in_specs=[
+                pl.BlockSpec((out_rows, in_rows), lambda c, s, lst, cnt: (0, 0)),
+                pl.BlockSpec((in_rows, out_rows), lambda c, s, lst, cnt: (0, 0)),
+                pl.BlockSpec(
+                    (blocks, None, parts, rows, inner), lambda c, s, lst, cnt: (0, c, 0, 0, lst[s])
+                ),
+                pl.BlockSpec(
+                    (None, parts, None, out_rows // parts, inner),
+                    lambda c, s, lst, cnt: (c, 0, s, 0, 0),
+                ),
+            ],
+            out_specs=pl.BlockSpec((None, None, in_rows, inner), lambda c, s, lst, cnt: (c, s, 0, 0)),
+        ),
+        out_shape=jax.ShapeDtypeStruct((chans, slots, in_rows, inner), jnp.bfloat16),
+        cost_estimate=pl.CostEstimate(
+            flops=flops, bytes_accessed=2 * chans * slots * (out_rows + 2 * in_rows) * inner,
+            transcendentals=0,
+        ),
+    )(own_list, own_count, kernel_mat, kernel_adj, gathered, own_data)
+
+
 def per_device(image, wavelet_dual, weights, kernels, vis_data, tile_list, tile_count):
     panel_rows, chan_count, grid_width = image.shape
     inner = tile_width
@@ -121,22 +173,18 @@
         .reshape(panel_rows, chan_count, 2, grid_width)
         .astype(bf)
     )
-    gathered = lax.all_gather(grid_panel, "vis", axis=0, tiled=True)
-    facet_rows = gathered.shape[0]
-    split_rows = gathered.reshape(facet_rows, chan_count, 2, outer, inner)
-    tiles = jnp.take(split_rows, own_list, axis=3)
+    panel_t = jnp.transpose(grid_panel, (1, 2, 0, 3))
+    gathered = lax.all_gather(panel_t, "vis", axis=0)
+    blocks = gathered.shape[0]
     stacked = kernel_blocks(kernels[0, 0])
-    predicted = jnp.einsum(
-        "omir,rcisn->cosmn", stacked, tiles, preferred_element_type=f32
-    )
+    out_rows, vis_rows = stacked.shape[0] * stacked.shape[1], stacked.shape[2] * blocks * panel_rows
+    kernel_mat = jnp.transpose(
+        stacked.reshape(2, -1, 2, blocks, panel_rows), (0, 1, 3, 2, 4)
+    ).reshape(out_rows, vis_rows)
+    kernel_adj = jnp.transpose(kernel_mat)
     own_data = vis_data[0, 0]
-    live_slots = (jnp.arange(slots_count, dtype=jnp.int32) < own_count)[None, None, :, None, None]
-    residual = jnp.where(live_slots, predicted - own_data.astype(f32), 0.0).astype(bf)
-    blocks = facet_rows // panel_rows
-    stacked5 = stacked.reshape(2, -1, 2, blocks, panel_rows)
-    partial = jnp.einsum(
-        "omivr,cosmn->iscvrn", stacked5, residual, preferred_element_type=f32
-    ).astype(bf)
+    partial = degrid_grid(own_list, own_count.reshape(1), kernel_mat, kernel_adj, gathered, own_data)
+    partial = partial.reshape(chan_count, slots_count, blocks, 2, panel_rows, inner)
     inner_index = jnp.arange(inner, dtype=jnp.int32)
     outer_index = jnp.arange(outer, dtype=jnp.int32)
     cos_in, sin_in = angle_table(inner_index, inner_index, inner)
@@ -146,11 +194,13 @@
     tw_s = sin_tw[None, :, None, None, :]
     inv_c = jnp.transpose(cos_sel).astype(bf)
     inv_s = jnp.transpose(sin_sel).astype(bf)
-    back_re = jnp.einsum("sa,scvrk->vacrk", inv_c, partial[0], preferred_element_type=f32) - jnp.einsum(
-        "sa,scvrk->vacrk", inv_s, partial[1], preferred_element_type=f32
-    )
-    back_im = jnp.einsum("sa,scvrk->vacrk", inv_s, partial[0], preferred_element_type=f32) + jnp.einsum(
-        "sa,scvrk->vacrk", inv_c, partial[1], preferred_element_type=f32
+    part_re = partial[:, :, :, 0]
+    part_im = partial[:, :, :, 1]
+    back_re = jnp.einsum("sa,csvrk->vacrk", inv_c, part_re, preferred_element_type=f32) - jnp.einsum(
+        "sa,csvrk->vacrk", inv_s, part_im, preferred_element_type=f32
+    )
+    back_im = jnp.einsum("sa,csvrk->vacrk", inv_s, part_re, preferred_element_type=f32) + jnp.einsum(
+        "sa,csvrk->vacrk", inv_c, part_im, preferred_element_type=f32
     )
     turned_re = (back_re * tw_c - back_im * tw_s).astype(bf)
     turned_im = (back_re * tw_s + back_im * tw_c).astype(bf)

time: 250 us -> 255 us (1.020)
  Pallas kernels: 0 us -> 47.4 us
  local copies, waits for them, and re-layouts: 55.5 us -> 14.7 us
  matrix products: 54.3 us -> 41.2 us
  waiting for transfers between devices: 110 us -> 122 us
    pallas_call x0 -> x1, Pallas kernels: none -> 47.4 us  [degrid_grid(): pl.pallas_call(degrid_body, grid_spec=pltpu.PrefetchScalarGridSpec(num_sc...]
    all_gather x1 -> x0, local copies, waits for them, and re-layouts: 14.5 us -> none  [per_device(): gathered = lax.all_gather(grid_panel, 'vis', axis=0, tiled=True)]
    dot_general x6 -> x4, matrix products: 39.2 us -> 26 us  [the longest x1 14.6 us: per_device(): jnp.einsum('sa,csvrk->vacrk', inv_s, part_re, preferred_element_type=f32)]
    unnamed x16 -> x19, local copies, waits for them, and re-layouts: 15.1 us -> 3.83 us
    reshape x1, local copies, waits for them, and re-layouts: 12 us -> 0.84 us  [per_device(): kernel_mat = jnp.transpose(stacked.reshape(2, -1, 2, blocks, panel_rows),...]
    all_gather x1, waiting for transfers between devices: 45.9 us -> 56.8 us  [per_device(): gathered = lax.all_gather(panel_t, 'vis', axis=0)]
    gather x1 -> x0, local copies, waits for them, and re-layouts: 6.42 us -> none  [per_device(): tiles = jnp.take(split_rows, own_list, axis=3)]
    slice x1, local copies, waits for them, and re-layouts: 0.11 us -> 2.74 us  [per_device(): part_im = partial[:, :, :, 1]]
  transfers between devices with their start and end apart: 5 -> 5, of which waited for: 5 -> 5; matrix products, arithmetic and copies ran while one was open for 5% -> 1% of each run, Pallas kernels for 0% -> 0%
where the time goes in v1:
time: 255 us; the launch traced here: 253 us
  waiting for transfers between devices  122 us (48%)
  Pallas kernels  47.4 us (19%)
  matrix products  41.2 us (16%)
  between operations  15 us (6%)
  local copies, waits for them, and re-layouts  14.7 us (6%)
  starting transfers between devices  7.82 us (3%)
  other arithmetic  5.08 us (2%)
    all_gather x1, waiting for transfers between devices, per_device(): gathered = lax.all_gather(panel_t, 'vis', axis=0)  56.8 us
    reduce_scatter x1, waiting for transfers between devices, per_device(): lax.psum_scatter(rows_part.astype(bf), 'vis', scatter_dimension=0, tiled=...  50.6 us
    pallas_call x1, Pallas kernels, degrid_grid(): pl.pallas_call(degrid_body, grid_spec=pltpu.PrefetchScalarGridSpec(num_sc...  47.4 us
    dot_general x1, matrix products, per_device(): jnp.einsum('sa,csvrk->vacrk', inv_s, part_re, preferred_element_type=f32)  14.6 us
    ppermute x2, waiting for transfers between devices, shifted(): lax.ppermute(value, axis, [(source, source + steps) for source in range(i...  11.1 us
    ppermute x2, starting transfers between devices, shifted(): lax.ppermute(value, axis, [(source, source + steps) for source in range(i...  6.53 us
  transfers between devices with their start and end apart: 5, of which 5 were waited for; matrix products, arithmetic and copies ran while one was open for 1% of the time, Pallas kernels for 0%

profile of v1, /device:TPU:24, one launch (start us, length us, event | category | flops | bytes accessed | tf_op | source)
XLA Modules:
  0.0 253.2 jit_solution(4515147926045056627)
XLA Ops:
  7.7 1.4 reshape_reshape.3
  13.2 1.1 fusion.23
  15.9 1.1 fusion.22
  18.9 1.1 copy.55
  22.0 56.8 %all-gather.3.cloned.1.call-done = bf16[64,2,8,4096]{3,2,1,0:T(8,128)(2,1)} async-done(((bf16[4,2,8,4096]{3,2,1,0:T(8,128)(2,1)}), bf16[64,2,8,4096]{3,2,1,0:T(8,128)(2,1)}) %all-gather.3.cloned.1.call-update) | async-done | bytes 8388624 | tf_op jit(solution)/shard_map/all_gather | solution.py:177
  78.8 47.4 %shard_map.86 = bf16[4,16,256,128]{3,2,1,0:T(8,128)(2,1)} custom-call(s32[16]{0:T(128)} %bitcast.116, s32[1]{0:T(128)} %bitcast.108.count_ref, bf16[512,256]{1,0:T(8,128)(2,1)} %copy.56.kmat_ref, bf16[256,512]{1,0:T(8,128)(2,1)} %bitcast.113, bf16[16,4,2,8,4096]{4,3,2,1,0:T(8,128)(2,1)} %bitcast.111, bf16[4,2,16,256,128]{4,3,2,1,0:T(8,128)(2,1)} %bitcast.110), custom_call_target="tpu_custom_call" | custom-call | flops 4294967296 | bytes 16777216 | tf_op jit(solution)/shard_map/pallas_call | solution.py:133
  126.1 2.7 %fusion.178 = (bf16[4,16,16,1,8,128]{5,4,3,2,1,0:T(8,128)(2,1)S(1)}, bf16[4,16,16,1,8,128]{5,4,3,2,1,0:T(8,128)(2,1)S(1)}) fusion(bf16[4,16,16,2,8,128]{5,4,3,2,1,0:T(8,128)(2,1)} %bitcast.109), kind=kLoop, calls=%fused_computation.208 | loop fusion | bytes 8388608 | tf_op jit(solution)/shard_map/slice | solution.py:198
  128.9 1.6 fusion.12
  130.5 4.9 %fusion.13 = f32[4,16,8,128,32]{3,4,2,1,0:T(8,128)} fusion(bf16[4,16,16,1,8,128]{5,4,3,2,1,0:T(8,128)(2,1)S(1)} %get-tuple-element.12, s32[16]{0:T(128)S(1)} %bitcast.118), kind=kOutput, calls=%fused_computation.18 | convolution fusion | flops 67116544 | bytes 10485824 | tf_op jit(solution)/shard_map/sa,csvrk->vacrk/dot_general | solution.py:199
  135.4 4.9 %fusion.11 = f32[4,16,8,128,32]{3,4,2,1,0:T(8,128)} fusion(bf16[4,16,16,1,8,128]{5,4,3,2,1,0:T(8,128)(2,1)S(1)} %get-tuple-element.13, s32[16]{0:T(128)S(1)} %bitcast.119), kind=kOutput, calls=%fused_computation.16 | convolution fusion | flops 67116544 | bytes 10485824 | tf_op jit(solution)/shard_map/sa,csvrk->vacrk/dot_general | solution.py:199
  140.3 14.6 %fusion.1 = (bf16[16,32,4,8,128]{4,1,3,0,2:T(8,128)(2,1)}, bf16[16,32,4,8,128]{4,1,3,0,2:T(8,128)(2,1)}) fusion(f32[32,128]{1,0:T(8,128)S(1)} %fusion.101, f32[32,128]{1,0:T(8,128)S(1)} %get-tuple-element.19, f32[4,16,8,128,32]{3,4,2,1,0:T(8,128)S(1)} %fusion.12, f32[4,16,8,128,32]{3,4,2,1,0:T(8,128)} %fusion.11, f32[4,16,8,128,32]{3,4,2,1,0:T(8,128)} %fusion.13, ...), kind=kOutput, calls=%fused_computation.3 | convolution fusion | flops 88088064 | bytes 35684416 | tf_op jit(solution)/shard_map/sa,csvrk->vacrk/dot_general | solution.py:202
  154.9 4.1 %fusion.4 = f32[16,32,4,8,128]{4,3,2,1,0:T(8,128)S(1)} fusion(bf16[16,32,4,8,128]{4,1,3,0,2:T(8,128)(2,1)} %get-tuple-element.11), kind=kOutput, calls=%fused_computation.9 | convolution fusion | flops 537133056 | bytes 12582912 | tf_op jit(solution)/shard_map/vacrk,kb->vacrb/dot_general | solution.py:209
  159.0 4.4 %subtract_convert_fusion = bf16[16,32,4,8,128]{4,3,2,1,0:T(8,128)(2,1)} fusion(f32[16,32,4,8,128]{4,3,2,1,0:T(8,128)S(1)} %fusion.4, bf16[16,32,4,8,128]{4,1,3,0,2:T(8,128)(2,1)S(1)} %copy-done.1), kind=kOutput, calls=%fused_computation.8 | convolution fusion | flops 541327360 | bytes 16777216 | tf_op jit(solution)/shard_map/vacrk,kb->vacrb/dot_general | solution.py:209
  164.9 1.9 collective-permute-start
  166.8 8.6 %collective-permute-done = bf16[3,4,4096]{2,0,1:T(4,128)(2,1)S(1)} collective-permute-done((bf16[3,4,4096]{2,0,1:T(4,128)(2,1)S(1)}, bf16[3,4,4096]{2,0,1:T(4,128)(2,1)S(1)}, u32[]{:S(2)}, u32[]{:S(2)}) %collective-permute-start) | collective-permute-done | bytes 98336 | tf_op jit(solution)/shard_map/ppermute | solution.py:28
  175.4 50.6 %reduce-scatter.2.cloned.1.call-done = bf16[1,32,4,8,128]{4,3,2,1,0:T(8,128)(2,1)} async-done(((bf16[16,32,4,8,128]{4,3,2,1,0:T(8,128)(2,1)}), bf16[1,32,4,8,128]{4,3,2,1,0:T(8,128)(2,1)}) %reduce-scatter.2.cloned.1.call-update) | async-done | bytes 262160 | tf_op jit(solution)/shard_map/reduce_scatter | solution.py:212
  228.7 1.7 multiply_subtract_fusion
  230.4 4.6 %collective-permute-start.1 = (bf16[3,4,4096]{2,0,1:T(4,128)(2,1)S(1)}, bf16[3,4,4096]{2,0,1:T(4,128)(2,1)S(1)}, u32[]{:S(2)}, u32[]{:S(2)}) collective-permute-start(bf16[3,4,4096]{2,0,1:T(4,128)(2,1)S(1)} %slice.126), channel_id=1, source_target_pairs={{2,0},{4,2},{6,4},{8,6},{10,8},{12,10},{14,12},{16,14},{18,16},{20... | collective-permute-start | bytes 294920 | tf_op jit(solution)/shard_map/ppermute | solution.py:28
  235.0 2.5 collective-permute-done.1
  237.5 1.7 multiply_reduce_fusion
  239.2 1.2 collective-permute-start.2
  240.4 1.1 copy.68
  241.5 3.5 %collective-permute-done.2 = bf16[8,4096]{1,0:T(8,128)(2,1)S(1)} collective-permute-done((bf16[8,4096]{1,0:T(8,128)(2,1)S(1)}, bf16[8,4096]{1,0:T(8,128)(2,1)S(1)}, u32[]{:S(2)}, u32[]{:S(2)}) %collective-permute-start.2) | collective-permute-done | bytes 65568 | tf_op jit(solution)/shard_map/ppermute | solution.py:235
  245.2 1.1 copy.69
  (49 shorter events, 13.5 us)
Async XLA Ops:
  7.2 71.6 %all-gather.3.cloned.1.call-start = ((), (), s32[]{:S(2)}) async-start(), calls=%async_computation.2 | async-start | bytes 8912896 | tf_op jit(solution)/shard_map/all_gather | solution.py:177
  14.8 5.2 %copy-start.5 = (bf16[1,1,2,256,128]{4,3,2,1,0:T(8,128)(2,1)S(1)}, bf16[1,1,2,256,128]{4,3,2,1,0:T(8,128)(2,1)}, u32[]{:S(2)}) copy-start(bf16[1,1,2,256,128]{4,3,2,1,0:T(8,128)(2,1)} %param.10) | copy-start | bytes 393220
  20.0 206.1 %reduce-scatter.2.cloned.1.call-start = ((), (), s32[]{:S(2)}) async-start(), calls=%async_computation.1 | async-start | bytes 4456448 | tf_op jit(solution)/shard_map/reduce_scatter | solution.py:212
  20.4 58.4 %copy-start.2 = (bf16[2,256,16,2,8]{1,4,0,3,2:T(8,128)(2,1)}, bf16[2,256,16,2,8]{1,4,0,3,2:T(8,128)(2,1)S(1)}, u32[]{:S(2)}) copy-start(bf16[2,256,16,2,8]{1,4,0,3,2:T(8,128)(2,1)S(1)} %copy.48) | copy-start | bytes 786436
  126.1 2.8 %copy-start.6 = (s32[1,1,16]{2,1,0:T(1,128)S(1)}, s32[1,1,16]{2,1,0:T(1,128)}, u32[]{:S(2)}) copy-start(s32[1,1,16]{2,1,0:T(1,128)} %param.12) | copy-start | bytes 196
  128.9 6.5 %copy-start = (bf16[4,16,16,1,8,128]{5,4,3,2,1,0:T(8,128)(2,1)}, bf16[4,16,16,1,8,128]{5,4,3,2,1,0:T(8,128)(2,1)S(1)}, u32[]{:S(2)}) copy-start(bf16[4,16,16,1,8,128]{5,4,3,2,1,0:T(8,128)(2,1)S(1)} %get-tuple-element.13) | copy-start | bytes 6291460
  154.9 4.1 %copy-start.1 = (bf16[16,32,4,8,128]{4,1,3,0,2:T(8,128)(2,1)S(1)}, bf16[16,32,4,8,128]{4,1,3,0,2:T(8,128)(2,1)}, u32[]{:S(2)}) copy-start(bf16[16,32,4,8,128]{4,1,3,0,2:T(8,128)(2,1)} %get-tuple-element.10) | copy-start | bytes 12582916
  163.5 1.0 copy-start.3
  164.9 10.5 %collective-permute-start = (bf16[3,4,4096]{2,0,1:T(4,128)(2,1)S(1)}, bf16[3,4,4096]{2,0,1:T(4,128)(2,1)S(1)}, u32[]{:S(2)}, u32[]{:S(2)}) collective-permute-start(bf16[3,4,4096]{2,0,1:T(4,128)(2,1)S(1)} %slice.127), channel_id=1, source_target_pairs={{0,2},{2,4},{4,6},{6,8},{8,10},{10,12},{12,14},{14,16},{16,18},{18... | collective-permute-start | bytes 294920 | tf_op jit(solution)/shard_map/ppermute | solution.py:28
  227.7 17.4 %copy-start.4 = (f32[8,4096]{1,0:T(8,128)S(1)}, f32[8,4096]{1,0:T(8,128)}, u32[]{:S(2)}) copy-start(f32[8,4096]{1,0:T(8,128)} %param.9) | copy-start | bytes 393220
  230.4 7.1 %collective-permute-start.1 = (bf16[3,4,4096]{2,0,1:T(4,128)(2,1)S(1)}, bf16[3,4,4096]{2,0,1:T(4,128)(2,1)S(1)}, u32[]{:S(2)}, u32[]{:S(2)}) collective-permute-start(bf16[3,4,4096]{2,0,1:T(4,128)(2,1)S(1)} %slice.126), channel_id=1, source_target_pairs={{2,0},{4,2},{6,4},{8,6},{10,8},{12,10},{14,12},{16,14},{18,16},{20... | collective-permute-start | bytes 294920 | tf_op jit(solution)/shard_map/ppermute | solution.py:28
  239.2 5.9 %collective-permute-start.2 = (bf16[8,4096]{1,0:T(8,128)(2,1)S(1)}, bf16[8,4096]{1,0:T(8,128)(2,1)S(1)}, u32[]{:S(2)}, u32[]{:S(2)}) collective-permute-start(bf16[8,4096]{1,0:T(8,128)(2,1)S(1)} %convert_element_type.114), channel_id=1, source_target_pairs={{0,1},{1,0},{2,3},{3,2},{4,5},{5,4},{6,7},{7,6},{8,9},{9,8},{10,11... | collective-permute-start | bytes 196616 | tf_op jit(solution)/shard_map/ppermute | solution.py:235
Sparse Core Ops, SparseCore 0:
  20.1 58.5 all-gather.2
  163.6 62.3 reduce-scatter.1

commit v2 on v1

--- a/solution.py
+++ b/solution.py
@@ -156,8 +156,26 @@
     )(own_list, own_count, kernel_mat, kernel_adj, gathered, own_data)
 
 
-def per_device(image, wavelet_dual, weights, kernels, vis_data, tile_list, tile_count):
+def chunk_grid(image):
     panel_rows, chan_count, grid_width = image.shape
+    inner = tile_width
+    outer = grid_width // inner
+    unit_scale = 1.0 / math.sqrt(grid_width)
+    bf = jnp.bfloat16
+    f32 = jnp.float32
+    image_rows = image.reshape(panel_rows * chan_count, grid_width)
+    grid_re, grid_im = fourier_rows(image_rows, jnp.zeros_like(image_rows), -1.0)
+    grid_panel = (
+        jnp.stack([grid_re, grid_im], axis=1)
+        .reshape(panel_rows, chan_count, 2, grid_width)
+        .astype(bf)
+    )
+    panel_t = jnp.transpose(grid_panel, (1, 2, 0, 3))
+    return lax.all_gather(panel_t, "vis", axis=0)
+
+
+def chunk_rows(gathered, kernels, own_data, tile_list, tile_count):
+    blocks, chan_count, parts, panel_rows, grid_width = gathered.shape
     inner = tile_width
     outer = grid_width // inner
     unit_scale = 1.0 / math.sqrt(grid_width)
@@ -166,15 +184,6 @@
     own_list = tile_list[0, 0]
     own_count = tile_count[0, 0]
     slots_count = own_list.shape[0]
-    image_rows = image.reshape(panel_rows * chan_count, grid_width)
-    grid_re, grid_im = fourier_rows(image_rows, jnp.zeros_like(image_rows), -1.0)
-    grid_panel = (
-        jnp.stack([grid_re, grid_im], axis=1)
-        .reshape(panel_rows, chan_count, 2, grid_width)
-        .astype(bf)
-    )
-    panel_t = jnp.transpose(grid_panel, (1, 2, 0, 3))
-    gathered = lax.all_gather(panel_t, "vis", axis=0)
     blocks = gathered.shape[0]
     stacked = kernel_blocks(kernels[0, 0])
     out_rows, vis_rows = stacked.shape[0] * stacked.shape[1], stacked.shape[2] * blocks * panel_rows
@@ -182,7 +191,6 @@
         stacked.reshape(2, -1, 2, blocks, panel_rows), (0, 1, 3, 2, 4)
     ).reshape(out_rows, vis_rows)
     kernel_adj = jnp.transpose(kernel_mat)
-    own_data = vis_data[0, 0]
     partial = degrid_grid(own_list, own_count.reshape(1), kernel_mat, kernel_adj, gathered, own_data)
     partial = partial.reshape(chan_count, slots_count, blocks, 2, panel_rows, inner)
     inner_index = jnp.arange(inner, dtype=jnp.int32)
@@ -209,11 +217,34 @@
     rows_part = jnp.einsum("vacrk,kb->vacrb", turned_re, out_c, preferred_element_type=f32) - jnp.einsum(
         "vacrk,kb->vacrb", turned_im, out_s, preferred_element_type=f32
     )
-    rows_sum = lax.psum_scatter(rows_part.astype(bf), "vis", scatter_dimension=0, tiled=True)
-    gradient = (
-        jnp.transpose(rows_sum[0].astype(f32), (2, 1, 3, 0))
-        .reshape(panel_rows, chan_count, grid_width)
-    )
+    return rows_part.astype(bf)
+
+
+def rows_gradient(rows_part):
+    rows_sum = lax.psum_scatter(rows_part, "vis", scatter_dimension=0, tiled=True)
+    outer, chan_count, panel_rows, inner = rows_sum.shape[1:]
+    return (
+        jnp.transpose(rows_sum[0].astype(jnp.float32), (2, 1, 3, 0))
+        .reshape(panel_rows, chan_count, outer * inner)
+    )
+
+
+def per_device(image, wavelet_dual, weights, kernels, vis_data, tile_list, tile_count):
+    panel_rows, chan_count, grid_width = image.shape
+    bf = jnp.bfloat16
+    f32 = jnp.float32
+    chunks = 2
+    width = chan_count // chunks
+    grids = [chunk_grid(image[:, part * width : (part + 1) * width]) for part in range(chunks)]
+    pieces = []
+    for part in range(chunks):
+        rows_part = chunk_rows(
+            grids[part], kernels, vis_data[0, 0, part * width : (part + 1) * width], tile_list, tile_count
+        )
+        if part + 1 < chunks:
+            rows_part, grids[part + 1] = lax.optimization_barrier((rows_part, grids[part + 1]))
+        pieces.append(rows_gradient(rows_part))
+    gradient = jnp.concatenate(pieces, axis=1)
     upper_rim = shifted(
         wavelet_dual[panel_rows - 3 :].astype(jnp.bfloat16), ("facet", "vis"), 1
     ).astype(jnp.float32)

time: 255 us -> 282 us (1.11)
  waiting for transfers between devices: 122 us -> 162 us
  matrix products: 41.2 us -> 25.3 us
  local copies, waits for them, and re-layouts: 14.7 us -> 24 us
  Pallas kernels: 47.4 us -> 42.9 us
    reduce_scatter x1 -> x2, waiting for transfers between devices: 50.6 us -> 108 us  [rows_gradient(): lax.psum_scatter(rows_part, 'vis', scatter_dimension=0, tiled=True)]
    dot_general x6 -> x12, matrix products: 34.5 us -> 17.9 us  [the longest x2 5.14 us: chunk_rows(): jnp.einsum('vacrk,kb->vacrb', turned_im, out_s, preferred_element_type=f32)]
    all_gather x1 -> x2, waiting for transfers between devices: 56.8 us -> 40.5 us  [chunk_grid(): return lax.all_gather(panel_t, 'vis', axis=0)]
    squeeze x0 -> x1, local copies, waits for them, and re-layouts: none -> 6.06 us  [per_device(): vis_data[0, 0, part * width:(part + 1) * width]]
    pallas_call x1 -> x2, Pallas kernels: 47.4 us -> 42.9 us  [degrid_grid(): pl.pallas_call(degrid_body, grid_spec=pltpu.PrefetchScalarGridSpec(num_sc...]
    transpose x2 -> x5, local copies, waits for them, and re-layouts: 1.1 us -> 4.1 us  [the longest x2 2.37 us: rows_gradient(): jnp.transpose(rows_sum[0].astype(jnp.float32), (2, 1, 3, 0))]
  transfers between devices with their start and end apart: 5 -> 7, of which waited for: 5 -> 7; matrix products, arithmetic and copies ran while one was open for 1% -> 10% of each run, Pallas kernels for 0% -> 8%
where the time goes in v2:
time: 282 us; the launch traced here: 281 us
  waiting for transfers between devices  162 us (57%)
  Pallas kernels  42.9 us (15%)
  matrix products  25.3 us (9%)
  local copies, waits for them, and re-layouts  24 us (9%)
  between operations  14.9 us (5%)
  starting transfers between devices  9.67 us (3%)
    reduce_scatter x2, waiting for transfers between devices, rows_gradient(): lax.psum_scatter(rows_part, 'vis', scatter_dimension=0, tiled=True)  108 us
    pallas_call x2, Pallas kernels, degrid_grid(): pl.pallas_call(degrid_body, grid_spec=pltpu.PrefetchScalarGridSpec(num_sc...  42.9 us
    all_gather x2, waiting for transfers between devices, chunk_grid(): return lax.all_gather(panel_t, 'vis', axis=0)  40.5 us
    ppermute x2, waiting for transfers between devices, shifted(): lax.ppermute(value, axis, [(source, source + steps) for source in range(i...  9.31 us
    ppermute x2, starting transfers between devices, shifted(): lax.ppermute(value, axis, [(source, source + steps) for source in range(i...  8.11 us
    squeeze x1, local copies, waits for them, and re-layouts, per_device(): vis_data[0, 0, part * width:(part + 1) * width]  6.06 us
  transfers between devices with their start and end apart: 7, of which 7 were waited for; matrix products, arithmetic and copies ran while one was open for 10% of the time, Pallas kernels for 8%

profile of v2, /device:TPU:24, one launch (start us, length us, event | category | flops | bytes accessed | tf_op | source)
XLA Modules:
  0.0 280.7 jit_solution(5248002828626051407)
XLA Ops:
  8.0 1.5 fusion.261
  24.6 6.1 %slice_bitcast_fusion = (bf16[2,2,16,256,128]{4,3,2,1,0:T(8,128)(2,1)}, bf16[2,2,16,256,128]{4,3,2,1,0:T(8,128)(2,1)}) fusion(bf16[1,1,4,2,16,256,128]{6,5,4,3,2,1,0:T(8,128)(2,1)} %param.11), kind=kLoop, calls=%fused_computation.17 | loop fusion | bytes 16777216 | tf_op jit(solution)/shard_map/squeeze | solution.py:242
  30.7 30.2 %all-gather.5.cloned.1.call-done = bf16[32,2,8,4096]{3,2,1,0:T(8,128)(2,1)} async-done(((bf16[2,2,8,4096]{3,2,1,0:T(8,128)(2,1)}), bf16[32,2,8,4096]{3,2,1,0:T(8,128)(2,1)}) %all-gather.5.cloned.1.call-update) | async-done | bytes 4194320 | tf_op jit(solution)/shard_map/all_gather | solution.py:174
  60.9 21.5 %shard_map.86 = bf16[2,16,256,128]{3,2,1,0:T(8,128)(2,1)} custom-call(s32[16]{0:T(128)} %bitcast.201, s32[1]{0:T(128)} %bitcast.188.count_ref, bf16[512,256]{1,0:T(8,128)(2,1)} %copy.58.kmat_ref, bf16[256,512]{1,0:T(8,128)(2,1)} %bitcast.193, bf16[16,2,2,8,4096]{4,3,2,1,0:T(8,128)(2,1)} %bitcast.195, bf16[2,2,16,256,128]{4,3,2,1,0:T(8,128)(2,1)} %get-tuple-element.19.vis_ref), custom_call_target="tpu_custom_call" | custom-call | flops 2147483648 | bytes 8388608 | tf_op jit(solution)/shard_map/pallas_call | solution.py:133
  82.4 1.8 fusion.260
  87.2 2.3 fusion.7
  90.6 2.6 subtract_convert_fusion.1
  93.2 10.3 %all-gather.7.cloned.1.call-done = bf16[32,2,8,4096]{3,2,1,0:T(8,128)(2,1)} async-done(((bf16[2,2,8,4096]{3,2,1,0:T(8,128)(2,1)}), bf16[32,2,8,4096]{3,2,1,0:T(8,128)(2,1)}) %all-gather.7.cloned.1.call-update) | async-done | bytes 4194320 | tf_op jit(solution)/shard_map/all_gather | solution.py:174
  103.5 21.5 %shard_map.87 = bf16[2,16,256,128]{3,2,1,0:T(8,128)(2,1)} custom-call(s32[16]{0:T(128)} %bitcast.202, s32[1]{0:T(128)} %bitcast.189.count_ref, bf16[512,256]{1,0:T(8,128)(2,1)} %copy.58.kmat_ref, bf16[256,512]{1,0:T(8,128)(2,1)} %bitcast.194, bf16[16,2,2,8,4096]{4,3,2,1,0:T(8,128)(2,1)} %bitcast.196, bf16[2,2,16,256,128]{4,3,2,1,0:T(8,128)(2,1)} %get-tuple-element.18.vis_ref), custom_call_target="tpu_custom_call" | custom-call | flops 2147483648 | bytes 8388608 | tf_op jit(solution)/shard_map/pallas_call | solution.py:133
  124.9 1.7 fusion.259
  129.7 2.3 fusion.3
  133.1 2.5 subtract_convert_fusion
  137.1 3.7 %collective-permute-start = (bf16[3,4,4096]{2,0,1:T(4,128)(2,1)S(1)}, bf16[3,4,4096]{2,0,1:T(4,128)(2,1)S(1)}, u32[]{:S(2)}, u32[]{:S(2)}) collective-permute-start(bf16[3,4,4096]{2,0,1:T(4,128)(2,1)S(1)} %slice.157), channel_id=1, source_target_pairs={{0,2},{2,4},{4,6},{6,8},{8,10},{10,12},{12,14},{14,16},{16,18},{18... | collective-permute-start | bytes 294920 | tf_op jit(solution)/shard_map/ppermute | solution.py:28
  140.8 6.8 %collective-permute-done = bf16[3,4,4096]{2,0,1:T(4,128)(2,1)S(1)} collective-permute-done((bf16[3,4,4096]{2,0,1:T(4,128)(2,1)S(1)}, bf16[3,4,4096]{2,0,1:T(4,128)(2,1)S(1)}, u32[]{:S(2)}, u32[]{:S(2)}) %collective-permute-start) | collective-permute-done | bytes 98336 | tf_op jit(solution)/shard_map/ppermute | solution.py:28
  147.6 49.0 %reduce-scatter.5.cloned.1.call-done = bf16[1,32,2,8,128]{4,3,2,1,0:T(8,128)(2,1)} async-done(((bf16[16,32,2,8,128]{4,3,2,1,0:T(8,128)(2,1)}), bf16[1,32,2,8,128]{4,3,2,1,0:T(8,128)(2,1)}) %reduce-scatter.5.cloned.1.call-update) | async-done | bytes 131088 | tf_op jit(solution)/shard_map/reduce_scatter | solution.py:224
  196.6 1.2 copy.72
  198.4 58.7 %reduce-scatter.3.cloned.1.call-done = bf16[1,32,2,8,128]{4,3,2,1,0:T(8,128)(2,1)} async-done(((bf16[16,32,2,8,128]{4,3,2,1,0:T(8,128)(2,1)}), bf16[1,32,2,8,128]{4,3,2,1,0:T(8,128)(2,1)}) %reduce-scatter.3.cloned.1.call-update) | async-done | bytes 131088 | tf_op jit(solution)/shard_map/reduce_scatter | solution.py:224
  257.1 1.2 copy.66
  259.5 4.4 %collective-permute-start.1 = (bf16[3,4,4096]{2,0,1:T(4,128)(2,1)S(1)}, bf16[3,4,4096]{2,0,1:T(4,128)(2,1)S(1)}, u32[]{:S(2)}, u32[]{:S(2)}) collective-permute-start(bf16[3,4,4096]{2,0,1:T(4,128)(2,1)S(1)} %slice.156), channel_id=1, source_target_pairs={{2,0},{4,2},{6,4},{8,6},{10,8},{12,10},{14,12},{16,14},{18,16},{20... | collective-permute-start | bytes 294920 | tf_op jit(solution)/shard_map/ppermute | solution.py:28
  263.9 2.5 collective-permute-done.1
  267.1 1.2 collective-permute-start.2
  268.3 1.1 copy.79
  269.4 3.5 %collective-permute-done.2 = bf16[8,4096]{1,0:T(8,128)(2,1)S(1)} collective-permute-done((bf16[8,4096]{1,0:T(8,128)(2,1)S(1)}, bf16[8,4096]{1,0:T(8,128)(2,1)S(1)}, u32[]{:S(2)}, u32[]{:S(2)}) %collective-permute-start.2) | collective-permute-done | bytes 65568 | tf_op jit(solution)/shard_map/ppermute | solution.py:266
  273.1 1.1 copy.80
  (79 shorter events, 27.1 us)
Async XLA Ops:
  7.2 53.7 %all-gather.5.cloned.1.call-start = ((), (), s32[]{:S(2)}) async-start(), calls=%async_computation.4 | async-start | bytes 4456448 | tf_op jit(solution)/shard_map/all_gather | solution.py:174
  15.9 87.6 %all-gather.7.cloned.1.call-start = ((), (), s32[]{:S(2)}) async-start(), calls=%async_computation.5 | async-start | bytes 4456448 | tf_op jit(solution)/shard_map/all_gather | solution.py:174
  16.6 6.0 %copy-start.4 = (bf16[1,1,2,256,128]{4,3,2,1,0:T(8,128)(2,1)S(1)}, bf16[1,1,2,256,128]{4,3,2,1,0:T(8,128)(2,1)}, u32[]{:S(2)}) copy-start(bf16[1,1,2,256,128]{4,3,2,1,0:T(8,128)(2,1)} %param.10) | copy-start | bytes 393220
  22.4 174.2 %reduce-scatter.5.cloned.1.call-start = ((), (), s32[]{:S(2)}) async-start(), calls=%async_computation.3 | async-start | bytes 2228224 | tf_op jit(solution)/shard_map/reduce_scatter | solution.py:224
  23.0 7.7 %copy-start = (bf16[2,256,16,2,8]{1,4,0,3,2:T(8,128)(2,1)}, bf16[2,256,16,2,8]{1,4,0,3,2:T(8,128)(2,1)S(1)}, u32[]{:S(2)}) copy-start(bf16[2,256,16,2,8]{1,4,0,3,2:T(8,128)(2,1)S(1)} %copy.54) | copy-start | bytes 786436
  82.4 1.8 copy-start.5
  124.9 1.7 copy-start.6
  135.7 1.0 copy-start.2
  135.7 123.1 %copy-start.1 = (f32[8,4,4096]{2,1,0:T(4,128)S(1)}, f32[8,4,4096]{2,1,0:T(4,128)}, u32[]{:S(2)}) copy-start(f32[8,4,4096]{2,1,0:T(4,128)} %param.7) | copy-start | bytes 1572868
  135.7 121.4 %reduce-scatter.3.cloned.1.call-start = ((), (), s32[]{:S(2)}) async-start(), calls=%async_computation.2 | async-start | bytes 2228224 | tf_op jit(solution)/shard_map/reduce_scatter | solution.py:224
  137.1 10.5 %collective-permute-start = (bf16[3,4,4096]{2,0,1:T(4,128)(2,1)S(1)}, bf16[3,4,4096]{2,0,1:T(4,128)(2,1)S(1)}, u32[]{:S(2)}, u32[]{:S(2)}) collective-permute-start(bf16[3,4,4096]{2,0,1:T(4,128)(2,1)S(1)} %slice.157), channel_id=1, source_target_pairs={{0,2},{2,4},{4,6},{6,8},{8,10},{10,12},{12,14},{14,16},{16,18},{18... | collective-permute-start | bytes 294920 | tf_op jit(solution)/shard_map/ppermute | solution.py:28
  197.8 75.1 %copy-start.3 = (f32[8,4096]{1,0:T(8,128)S(1)}, f32[8,4096]{1,0:T(8,128)}, u32[]{:S(2)}) copy-start(f32[8,4096]{1,0:T(8,128)} %param.9) | copy-start | bytes 393220
  259.5 6.9 %collective-permute-start.1 = (bf16[3,4,4096]{2,0,1:T(4,128)(2,1)S(1)}, bf16[3,4,4096]{2,0,1:T(4,128)(2,1)S(1)}, u32[]{:S(2)}, u32[]{:S(2)}) collective-permute-start(bf16[3,4,4096]{2,0,1:T(4,128)(2,1)S(1)} %slice.156), channel_id=1, source_target_pairs={{2,0},{4,2},{6,4},{8,6},{10,8},{12,10},{14,12},{16,14},{18,16},{20... | collective-permute-start | bytes 294920 | tf_op jit(solution)/shard_map/ppermute | solution.py:28
  267.1 5.9 %collective-permute-start.2 = (bf16[8,4096]{1,0:T(8,128)(2,1)S(1)}, bf16[8,4096]{1,0:T(8,128)(2,1)S(1)}, u32[]{:S(2)}, u32[]{:S(2)}) collective-permute-start(bf16[8,4096]{1,0:T(8,128)(2,1)S(1)} %convert_element_type.178), channel_id=1, source_target_pairs={{0,1},{1,0},{2,3},{3,2},{4,5},{5,4},{6,7},{7,6},{8,9},{9,8},{10,11... | collective-permute-start | bytes 196616 | tf_op jit(solution)/shard_map/ppermute | solution.py:266
Sparse Core Ops, SparseCore 0:
  16.0 44.8 all-gather.4
  62.7 40.7 all-gather.6
  135.8 60.7 reduce-scatter.4
  199.0 57.9 reduce-scatter.2

commit v3 on v1

--- a/solution.py
+++ b/solution.py
@@ -106,27 +106,39 @@
     )
 
 
-def degrid_body(list_ref, count_ref, kmat_ref, kadj_ref, grid_ref, vis_ref, out_ref):
-    slot = pl.program_id(1)
-
-    @pl.when(slot < count_ref[0])
-    def _():
-        rows = grid_ref.shape[0] * grid_ref.shape[1] * grid_ref.shape[2]
-        tile = grid_ref[...].astype(jnp.float32).reshape(rows, grid_ref.shape[3]).astype(jnp.bfloat16)
-        predicted = jnp.dot(kmat_ref[...], tile, preferred_element_type=jnp.float32)
-        measured = vis_ref[...].astype(jnp.float32).reshape(predicted.shape)
-        residual = (predicted - measured).astype(jnp.bfloat16)
-        gridded = jnp.dot(kadj_ref[...], residual, preferred_element_type=jnp.float32)
-        out_ref[...] = gridded.astype(out_ref.dtype)
-
-    @pl.when(slot >= count_ref[0])
-    def _():
-        out_ref[...] = jnp.zeros_like(out_ref)
+def degrid_body(list_ref, count_ref, kmat_ref, kadj_ref, *refs):
+    tile_refs, vis_ref, out_ref = refs[:-2], refs[-2], refs[-1]
+    group = len(tile_refs)
+    step = pl.program_id(1)
+    for place, grid_ref in enumerate(tile_refs):
+        slot = step * group + place
+
+        @pl.when(slot < count_ref[0])
+        def _():
+            rows = grid_ref.shape[0] * grid_ref.shape[1] * grid_ref.shape[2]
+            tile = grid_ref[...].astype(jnp.float32).reshape(rows, grid_ref.shape[3]).astype(jnp.bfloat16)
+            predicted = jnp.dot(kmat_ref[...], tile, preferred_element_type=jnp.float32)
+            measured = vis_ref[:, place].astype(jnp.float32).reshape(predicted.shape)
+            residual = (predicted - measured).astype(jnp.bfloat16)
+            gridded = jnp.dot(kadj_ref[...], residual, preferred_element_type=jnp.float32)
+            out_ref[place] = gridded.astype(out_ref.dtype)
+
+        @pl.when(slot >= count_ref[0])
+        def _():
+            out_ref[place] = jnp.zeros(out_ref.shape[1:], out_ref.dtype)
+
+
+def tile_spec(blocks, parts, rows, inner, group, place):
+    return pl.BlockSpec(
+        (blocks, None, parts, rows, inner),
+        lambda c, s, lst, cnt: (0, c, 0, 0, lst[s * group + place]),
+    )
 
 
 def degrid_grid(own_list, own_count, kernel_mat, kernel_adj, gathered, own_data):
     blocks, chans, parts, rows, width = gathered.shape
     slots = own_list.shape[0]
+    group = 4
     out_rows, in_rows = kernel_mat.shape
     inner = tile_width
     flops = 4 * out_rows * in_rows * inner * chans * slots
@@ -134,26 +146,26 @@
         degrid_body,
         grid_spec=pltpu.PrefetchScalarGridSpec(
             num_scalar_prefetch=2,
-            grid=(chans, slots),
+            grid=(chans, slots // group),
             in_specs=[
                 pl.BlockSpec((out_rows, in_rows), lambda c, s, lst, cnt: (0, 0)),
                 pl.BlockSpec((in_rows, out_rows), lambda c, s, lst, cnt: (0, 0)),
+            ]
+            + [tile_spec(blocks, parts, rows, inner, group, place) for place in range(group)]
+            + [
                 pl.BlockSpec(
-                    (blocks, None, parts, rows, inner), lambda c, s, lst, cnt: (0, c, 0, 0, lst[s])
-                ),
-                pl.BlockSpec(
-                    (None, parts, None, out_rows // parts, inner),
+                    (None, parts, group, out_rows // parts, inner),
                     lambda c, s, lst, cnt: (c, 0, s, 0, 0),
                 ),
             ],
-            out_specs=pl.BlockSpec((None, None, in_rows, inner), lambda c, s, lst, cnt: (c, s, 0, 0)),
+            out_specs=pl.BlockSpec((None, group, in_rows, inner), lambda c, s, lst, cnt: (c, s, 0, 0)),
         ),
         out_shape=jax.ShapeDtypeStruct((chans, slots, in_rows, inner), jnp.bfloat16),
         cost_estimate=pl.CostEstimate(
             flops=flops, bytes_accessed=2 * chans * slots * (out_rows + 2 * in_rows) * inner,
             transcendentals=0,
         ),
-    )(own_list, own_count, kernel_mat, kernel_adj, gathered, own_data)
+    )(own_list, own_count, kernel_mat, kernel_adj, *([gathered] * group), own_data)
 
 
 def per_device(image, wavelet_dual, weights, kernels, vis_data, tile_list, tile_count):

time: 255 us -> 238 us (0.933)
  Pallas kernels: 47.4 us -> 31 us
    pallas_call x1, Pallas kernels: 47.4 us -> 31 us  [degrid_grid(): pl.pallas_call(degrid_body, grid_spec=pltpu.PrefetchScalarGridSpec(num_sc...]
where the time goes in v3:
time: 238 us; the launch traced here: 237 us
  waiting for transfers between devices  122 us (51%)
  matrix products  41.2 us (17%)
  Pallas kernels  31 us (13%)
  between operations  15 us (6%)
  local copies, waits for them, and re-layouts  14.7 us (6%)
  starting transfers between devices  7.51 us (3%)
  other arithmetic  5.08 us (2%)
    all_gather x1, waiting for transfers between devices, per_device(): gathered = lax.all_gather(panel_t, 'vis', axis=0)  56.8 us
    reduce_scatter x1, waiting for transfers between devices, per_device(): lax.psum_scatter(rows_part.astype(bf), 'vis', scatter_dimension=0, tiled=...  51 us
    pallas_call x1, Pallas kernels, degrid_grid(): pl.pallas_call(degrid_body, grid_spec=pltpu.PrefetchScalarGridSpec(num_sc...  31 us
    dot_general x1, matrix products, per_device(): jnp.einsum('sa,csvrk->vacrk', inv_s, part_re, preferred_element_type=f32)  14.6 us
    ppermute x2, waiting for transfers between devices, shifted(): lax.ppermute(value, axis, [(source, source + steps) for source in range(i...  11.1 us
    ppermute x2, starting transfers between devices, shifted(): lax.ppermute(value, axis, [(source, source + steps) for source in range(i...  6.23 us
    dot_general x1, matrix products, per_device(): jnp.einsum('sa,csvrk->vacrk', inv_s, part_im, preferred_element_type=f32)  4.88 us
    dot_general x1, matrix products, per_device(): jnp.einsum('sa,csvrk->vacrk', inv_c, part_re, preferred_element_type=f32)  4.86 us
  transfers between devices with their start and end apart: 5, of which 5 were waited for; matrix products, arithmetic and copies ran while one was open for 1% of the time, Pallas kernels for 0%

profile of v3, /device:TPU:24, one launch (start us, length us, event | category | flops | bytes accessed | tf_op | source)
XLA Modules:
  0.0 236.9 jit_solution(2568097419308656120)
XLA Ops:
  7.7 1.4 reshape_reshape.3
  13.2 1.1 fusion.23
  15.9 1.1 fusion.22
  18.9 1.1 copy.55
  22.0 56.8 %all-gather.3.cloned.1.call-done = bf16[64,2,8,4096]{3,2,1,0:T(8,128)(2,1)} async-done(((bf16[4,2,8,4096]{3,2,1,0:T(8,128)(2,1)}), bf16[64,2,8,4096]{3,2,1,0:T(8,128)(2,1)}) %all-gather.3.cloned.1.call-update) | async-done | bytes 8388624 | tf_op jit(solution)/shard_map/all_gather | solution.py:189
  78.8 31.0 %shard_map.86 = bf16[4,16,256,128]{3,2,1,0:T(8,128)(2,1)} custom-call(s32[16]{0:T(128)} %bitcast.119, s32[1]{0:T(128)} %bitcast.108.count_ref, bf16[512,256]{1,0:T(8,128)(2,1)} %copy.56.kmat_ref, bf16[256,512]{1,0:T(8,128)(2,1)} %bitcast.116, bf16[16,4,2,8,4096]{4,3,2,1,0:T(8,128)(2,1)} %bitcast.109, bf16[16,4,2,8,4096]{4,3,2,1,0:T(8,128)(2,1)} %bitcast.110, ...), custom_call_target="tpu_custom_call" | custom-call | flops 4294967296 | bytes 16777216 | tf_op jit(solution)/shard_map/pallas_call | solution.py:145
  109.8 2.7 %fusion.178 = (bf16[4,16,16,1,8,128]{5,4,3,2,1,0:T(8,128)(2,1)S(1)}, bf16[4,16,16,1,8,128]{5,4,3,2,1,0:T(8,128)(2,1)S(1)}) fusion(bf16[4,16,16,2,8,128]{5,4,3,2,1,0:T(8,128)(2,1)} %bitcast.113), kind=kLoop, calls=%fused_computation.208 | loop fusion | bytes 8388608 | tf_op jit(solution)/shard_map/slice | solution.py:210
  112.5 1.6 fusion.12
  114.2 4.9 %fusion.13 = f32[4,16,8,128,32]{3,4,2,1,0:T(8,128)} fusion(bf16[4,16,16,1,8,128]{5,4,3,2,1,0:T(8,128)(2,1)S(1)} %get-tuple-element.12, s32[16]{0:T(128)S(1)} %bitcast.121), kind=kOutput, calls=%fused_computation.18 | convolution fusion | flops 67116544 | bytes 10485824 | tf_op jit(solution)/shard_map/sa,csvrk->vacrk/dot_general | solution.py:211
  119.0 4.9 %fusion.11 = f32[4,16,8,128,32]{3,4,2,1,0:T(8,128)} fusion(bf16[4,16,16,1,8,128]{5,4,3,2,1,0:T(8,128)(2,1)S(1)} %get-tuple-element.13, s32[16]{0:T(128)S(1)} %bitcast.122), kind=kOutput, calls=%fused_computation.16 | convolution fusion | flops 67116544 | bytes 10485824 | tf_op jit(solution)/shard_map/sa,csvrk->vacrk/dot_general | solution.py:211
  123.9 14.6 %fusion.1 = (bf16[16,32,4,8,128]{4,1,3,0,2:T(8,128)(2,1)}, bf16[16,32,4,8,128]{4,1,3,0,2:T(8,128)(2,1)}) fusion(f32[32,128]{1,0:T(8,128)S(1)} %fusion.101, f32[32,128]{1,0:T(8,128)S(1)} %get-tuple-element.19, f32[4,16,8,128,32]{3,4,2,1,0:T(8,128)S(1)} %fusion.12, f32[4,16,8,128,32]{3,4,2,1,0:T(8,128)} %fusion.11, f32[4,16,8,128,32]{3,4,2,1,0:T(8,128)} %fusion.13, ...), kind=kOutput, calls=%fused_computation.3 | convolution fusion | flops 88088064 | bytes 35684416 | tf_op jit(solution)/shard_map/sa,csvrk->vacrk/dot_general | solution.py:214
  138.5 4.1 %fusion.4 = f32[16,32,4,8,128]{4,3,2,1,0:T(8,128)S(1)} fusion(bf16[16,32,4,8,128]{4,1,3,0,2:T(8,128)(2,1)} %get-tuple-element.11), kind=kOutput, calls=%fused_computation.9 | convolution fusion | flops 537133056 | bytes 12582912 | tf_op jit(solution)/shard_map/vacrk,kb->vacrb/dot_general | solution.py:221
  142.7 4.4 %subtract_convert_fusion = bf16[16,32,4,8,128]{4,3,2,1,0:T(8,128)(2,1)} fusion(f32[16,32,4,8,128]{4,3,2,1,0:T(8,128)S(1)} %fusion.4, bf16[16,32,4,8,128]{4,1,3,0,2:T(8,128)(2,1)S(1)} %copy-done.1), kind=kOutput, calls=%fused_computation.8 | convolution fusion | flops 541327360 | bytes 16777216 | tf_op jit(solution)/shard_map/vacrk,kb->vacrb/dot_general | solution.py:221
  148.5 1.9 collective-permute-start
  150.4 8.6 %collective-permute-done = bf16[3,4,4096]{2,0,1:T(4,128)(2,1)S(1)} collective-permute-done((bf16[3,4,4096]{2,0,1:T(4,128)(2,1)S(1)}, bf16[3,4,4096]{2,0,1:T(4,128)(2,1)S(1)}, u32[]{:S(2)}, u32[]{:S(2)}) %collective-permute-start) | collective-permute-done | bytes 98336 | tf_op jit(solution)/shard_map/ppermute | solution.py:28
  159.0 51.0 %reduce-scatter.2.cloned.1.call-done = bf16[1,32,4,8,128]{4,3,2,1,0:T(8,128)(2,1)} async-done(((bf16[16,32,4,8,128]{4,3,2,1,0:T(8,128)(2,1)}), bf16[1,32,4,8,128]{4,3,2,1,0:T(8,128)(2,1)}) %reduce-scatter.2.cloned.1.call-update) | async-done | bytes 262160 | tf_op jit(solution)/shard_map/reduce_scatter | solution.py:224
  212.7 1.7 multiply_subtract_fusion
  214.4 4.3 %collective-permute-start.1 = (bf16[3,4,4096]{2,0,1:T(4,128)(2,1)S(1)}, bf16[3,4,4096]{2,0,1:T(4,128)(2,1)S(1)}, u32[]{:S(2)}, u32[]{:S(2)}) collective-permute-start(bf16[3,4,4096]{2,0,1:T(4,128)(2,1)S(1)} %slice.126), channel_id=1, source_target_pairs={{2,0},{4,2},{6,4},{8,6},{10,8},{12,10},{14,12},{16,14},{18,16},{20... | collective-permute-start | bytes 294920 | tf_op jit(solution)/shard_map/ppermute | solution.py:28
  218.7 2.5 %collective-permute-done.1 = bf16[3,4,4096]{2,0,1:T(4,128)(2,1)S(1)} collective-permute-done((bf16[3,4,4096]{2,0,1:T(4,128)(2,1)S(1)}, bf16[3,4,4096]{2,0,1:T(4,128)(2,1)S(1)}, u32[]{:S(2)}, u32[]{:S(2)}) %collective-permute-start.1) | collective-permute-done | bytes 98336 | tf_op jit(solution)/shard_map/ppermute | solution.py:28
  221.2 1.7 multiply_reduce_fusion
  222.9 1.2 collective-permute-start.2
  224.1 1.1 copy.68
  225.3 3.5 %collective-permute-done.2 = bf16[8,4096]{1,0:T(8,128)(2,1)S(1)} collective-permute-done((bf16[8,4096]{1,0:T(8,128)(2,1)S(1)}, bf16[8,4096]{1,0:T(8,128)(2,1)S(1)}, u32[]{:S(2)}, u32[]{:S(2)}) %collective-permute-start.2) | collective-permute-done | bytes 65568 | tf_op jit(solution)/shard_map/ppermute | solution.py:247
  228.9 1.1 copy.69
  (49 shorter events, 13.5 us)
Async XLA Ops:
  7.2 71.6 %all-gather.3.cloned.1.call-start = ((), (), s32[]{:S(2)}) async-start(), calls=%async_computation.2 | async-start | bytes 8912896 | tf_op jit(solution)/shard_map/all_gather | solution.py:189
  14.8 5.2 %copy-start.5 = (bf16[1,1,2,256,128]{4,3,2,1,0:T(8,128)(2,1)S(1)}, bf16[1,1,2,256,128]{4,3,2,1,0:T(8,128)(2,1)}, u32[]{:S(2)}) copy-start(bf16[1,1,2,256,128]{4,3,2,1,0:T(8,128)(2,1)} %param.10) | copy-start | bytes 393220
  20.0 190.1 %reduce-scatter.2.cloned.1.call-start = ((), (), s32[]{:S(2)}) async-start(), calls=%async_computation.1 | async-start | bytes 4456448 | tf_op jit(solution)/shard_map/reduce_scatter | solution.py:224
  20.4 58.4 %copy-start.2 = (bf16[2,256,16,2,8]{1,4,0,3,2:T(8,128)(2,1)}, bf16[2,256,16,2,8]{1,4,0,3,2:T(8,128)(2,1)S(1)}, u32[]{:S(2)}) copy-start(bf16[2,256,16,2,8]{1,4,0,3,2:T(8,128)(2,1)S(1)} %copy.48) | copy-start | bytes 786436
  109.8 2.8 %copy-start.6 = (s32[1,1,16]{2,1,0:T(1,128)S(1)}, s32[1,1,16]{2,1,0:T(1,128)}, u32[]{:S(2)}) copy-start(s32[1,1,16]{2,1,0:T(1,128)} %param.12) | copy-start | bytes 196
  112.5 6.5 %copy-start = (bf16[4,16,16,1,8,128]{5,4,3,2,1,0:T(8,128)(2,1)}, bf16[4,16,16,1,8,128]{5,4,3,2,1,0:T(8,128)(2,1)S(1)}, u32[]{:S(2)}) copy-start(bf16[4,16,16,1,8,128]{5,4,3,2,1,0:T(8,128)(2,1)S(1)} %get-tuple-element.13) | copy-start | bytes 6291460
  138.5 4.1 %copy-start.1 = (bf16[16,32,4,8,128]{4,1,3,0,2:T(8,128)(2,1)S(1)}, bf16[16,32,4,8,128]{4,1,3,0,2:T(8,128)(2,1)}, u32[]{:S(2)}) copy-start(bf16[16,32,4,8,128]{4,1,3,0,2:T(8,128)(2,1)} %get-tuple-element.10) | copy-start | bytes 12582916
  147.1 1.0 copy-start.3
  148.5 10.5 %collective-permute-start = (bf16[3,4,4096]{2,0,1:T(4,128)(2,1)S(1)}, bf16[3,4,4096]{2,0,1:T(4,128)(2,1)S(1)}, u32[]{:S(2)}, u32[]{:S(2)}) collective-permute-start(bf16[3,4,4096]{2,0,1:T(4,128)(2,1)S(1)} %slice.127), channel_id=1, source_target_pairs={{0,2},{2,4},{4,6},{6,8},{8,10},{10,12},{12,14},{14,16},{16,18},{18... | collective-permute-start | bytes 294920 | tf_op jit(solution)/shard_map/ppermute | solution.py:28
  211.7 17.1 %copy-start.4 = (f32[8,4096]{1,0:T(8,128)S(1)}, f32[8,4096]{1,0:T(8,128)}, u32[]{:S(2)}) copy-start(f32[8,4096]{1,0:T(8,128)} %param.9) | copy-start | bytes 393220
  214.4 6.8 %collective-permute-start.1 = (bf16[3,4,4096]{2,0,1:T(4,128)(2,1)S(1)}, bf16[3,4,4096]{2,0,1:T(4,128)(2,1)S(1)}, u32[]{:S(2)}, u32[]{:S(2)}) collective-permute-start(bf16[3,4,4096]{2,0,1:T(4,128)(2,1)S(1)} %slice.126), channel_id=1, source_target_pairs={{2,0},{4,2},{6,4},{8,6},{10,8},{12,10},{14,12},{16,14},{18,16},{20... | collective-permute-start | bytes 294920 | tf_op jit(solution)/shard_map/ppermute | solution.py:28
  222.9 5.9 %collective-permute-start.2 = (bf16[8,4096]{1,0:T(8,128)(2,1)S(1)}, bf16[8,4096]{1,0:T(8,128)(2,1)S(1)}, u32[]{:S(2)}, u32[]{:S(2)}) collective-permute-start(bf16[8,4096]{1,0:T(8,128)(2,1)S(1)} %convert_element_type.114), channel_id=1, source_target_pairs={{0,1},{1,0},{2,3},{3,2},{4,5},{5,4},{6,7},{7,6},{8,9},{9,8},{10,11... | collective-permute-start | bytes 196616 | tf_op jit(solution)/shard_map/ppermute | solution.py:247
Sparse Core Ops, SparseCore 0:
  20.1 58.5 all-gather.2
  147.2 62.7 reduce-scatter.1

commit v4 on v3

--- a/solution.py
+++ b/solution.py
@@ -138,7 +138,7 @@
 def degrid_grid(own_list, own_count, kernel_mat, kernel_adj, gathered, own_data):
     blocks, chans, parts, rows, width = gathered.shape
     slots = own_list.shape[0]
-    group = 4
+    group = 8
     out_rows, in_rows = kernel_mat.shape
     inner = tile_width
     flops = 4 * out_rows * in_rows * inner * chans * slots

time: 238 us -> 238 us (level)
  waiting for transfers between devices: 122 us -> 137 us
  Pallas kernels: 31 us -> 17.1 us
    pallas_call x1, Pallas kernels: 31 us -> 17.1 us  [degrid_grid(): pl.pallas_call(degrid_body, grid_spec=pltpu.PrefetchScalarGridSpec(num_sc...]
    reduce_scatter x1, waiting for transfers between devices: 51 us -> 64.3 us  [per_device(): lax.psum_scatter(rows_part.astype(bf), 'vis', scatter_dimension=0, tiled=...]
where the time goes in v4:
time: 238 us
  waiting for transfers between devices  137 us (58%)
  matrix products  41.2 us (17%)
  Pallas kernels  17.1 us (7%)
  between operations  15 us (6%)
  local copies, waits for them, and re-layouts  14.7 us (6%)
  starting transfers between devices  8.22 us (3%)
  other arithmetic  5.08 us (2%)
    reduce_scatter x1, waiting for transfers between devices, per_device(): lax.psum_scatter(rows_part.astype(bf), 'vis', scatter_dimension=0, tiled=...  64.3 us
    all_gather x1, waiting for transfers between devices, per_device(): gathered = lax.all_gather(panel_t, 'vis', axis=0)  56.6 us
    pallas_call x1, Pallas kernels, degrid_grid(): pl.pallas_call(degrid_body, grid_spec=pltpu.PrefetchScalarGridSpec(num_sc...  17.1 us
    dot_general x1, matrix products, per_device(): jnp.einsum('sa,csvrk->vacrk', inv_s, part_re, preferred_element_type=f32)  14.6 us
    ppermute x2, waiting for transfers between devices, shifted(): lax.ppermute(value, axis, [(source, source + steps) for source in range(i...  12.1 us
    ppermute x2, starting transfers between devices, shifted(): lax.ppermute(value, axis, [(source, source + steps) for source in range(i...  6.75 us
    dot_general x1, matrix products, per_device(): jnp.einsum('sa,csvrk->vacrk', inv_s, part_im, preferred_element_type=f32)  4.88 us
    dot_general x1, matrix products, per_device(): jnp.einsum('sa,csvrk->vacrk', inv_c, part_re, preferred_element_type=f32)  4.86 us
  transfers between devices with their start and end apart: 5, of which 5 were waited for; matrix products, arithmetic and copies ran while one was open for 1% of the time, Pallas kernels for 0%

profile of v4, /device:TPU:24, one launch (start us, length us, event | category | flops | bytes accessed | tf_op | source)
XLA Modules:
  0.0 237.8 jit_solution(7090298381935245924)
XLA Ops:
  7.7 1.4 reshape_reshape.3
  13.2 1.1 fusion.23
  15.9 1.1 fusion.22
  18.9 1.1 copy.55
  22.1 56.6 %all-gather.3.cloned.1.call-done = bf16[64,2,8,4096]{3,2,1,0:T(8,128)(2,1)} async-done(((bf16[4,2,8,4096]{3,2,1,0:T(8,128)(2,1)}), bf16[64,2,8,4096]{3,2,1,0:T(8,128)(2,1)}) %all-gather.3.cloned.1.call-update) | async-done | bytes 8388624 | tf_op jit(solution)/shard_map/all_gather | solution.py:189
  78.8 17.1 %shard_map.86 = bf16[4,16,256,128]{3,2,1,0:T(8,128)(2,1)} custom-call(s32[16]{0:T(128)} %bitcast.123, s32[1]{0:T(128)} %bitcast.108.count_ref, bf16[512,256]{1,0:T(8,128)(2,1)} %copy.56.kmat_ref, bf16[256,512]{1,0:T(8,128)(2,1)} %bitcast.120, bf16[16,4,2,8,4096]{4,3,2,1,0:T(8,128)(2,1)} %bitcast.109, bf16[16,4,2,8,4096]{4,3,2,1,0:T(8,128)(2,1)} %bitcast.110, ...), custom_call_target="tpu_custom_call" | custom-call | flops 4294967296 | bytes 16777216 | tf_op jit(solution)/shard_map/pallas_call | solution.py:145
  95.9 2.7 %fusion.178 = (bf16[4,16,16,1,8,128]{5,4,3,2,1,0:T(8,128)(2,1)S(1)}, bf16[4,16,16,1,8,128]{5,4,3,2,1,0:T(8,128)(2,1)S(1)}) fusion(bf16[4,16,16,2,8,128]{5,4,3,2,1,0:T(8,128)(2,1)} %bitcast.117), kind=kLoop, calls=%fused_computation.208 | loop fusion | bytes 8388608 | tf_op jit(solution)/shard_map/slice | solution.py:210
  98.7 1.6 fusion.12
  100.3 4.9 %fusion.13 = f32[4,16,8,128,32]{3,4,2,1,0:T(8,128)} fusion(bf16[4,16,16,1,8,128]{5,4,3,2,1,0:T(8,128)(2,1)S(1)} %get-tuple-element.12, s32[16]{0:T(128)S(1)} %bitcast.125), kind=kOutput, calls=%fused_computation.18 | convolution fusion | flops 67116544 | bytes 10485824 | tf_op jit(solution)/shard_map/sa,csvrk->vacrk/dot_general | solution.py:211
  105.2 4.9 %fusion.11 = f32[4,16,8,128,32]{3,4,2,1,0:T(8,128)} fusion(bf16[4,16,16,1,8,128]{5,4,3,2,1,0:T(8,128)(2,1)S(1)} %get-tuple-element.13, s32[16]{0:T(128)S(1)} %bitcast.126), kind=kOutput, calls=%fused_computation.16 | convolution fusion | flops 67116544 | bytes 10485824 | tf_op jit(solution)/shard_map/sa,csvrk->vacrk/dot_general | solution.py:211
  110.0 14.6 %fusion.1 = (bf16[16,32,4,8,128]{4,1,3,0,2:T(8,128)(2,1)}, bf16[16,32,4,8,128]{4,1,3,0,2:T(8,128)(2,1)}) fusion(f32[32,128]{1,0:T(8,128)S(1)} %fusion.101, f32[32,128]{1,0:T(8,128)S(1)} %get-tuple-element.19, f32[4,16,8,128,32]{3,4,2,1,0:T(8,128)S(1)} %fusion.12, f32[4,16,8,128,32]{3,4,2,1,0:T(8,128)} %fusion.11, f32[4,16,8,128,32]{3,4,2,1,0:T(8,128)} %fusion.13, ...), kind=kOutput, calls=%fused_computation.3 | convolution fusion | flops 88088064 | bytes 35684416 | tf_op jit(solution)/shard_map/sa,csvrk->vacrk/dot_general | solution.py:214
  124.6 4.1 %fusion.4 = f32[16,32,4,8,128]{4,3,2,1,0:T(8,128)S(1)} fusion(bf16[16,32,4,8,128]{4,1,3,0,2:T(8,128)(2,1)} %get-tuple-element.11), kind=kOutput, calls=%fused_computation.9 | convolution fusion | flops 537133056 | bytes 12582912 | tf_op jit(solution)/shard_map/vacrk,kb->vacrb/dot_general | solution.py:221
  128.8 4.4 %subtract_convert_fusion = bf16[16,32,4,8,128]{4,3,2,1,0:T(8,128)(2,1)} fusion(f32[16,32,4,8,128]{4,3,2,1,0:T(8,128)S(1)} %fusion.4, bf16[16,32,4,8,128]{4,1,3,0,2:T(8,128)(2,1)S(1)} %copy-done.1), kind=kOutput, calls=%fused_computation.8 | convolution fusion | flops 541327360 | bytes 16777216 | tf_op jit(solution)/shard_map/vacrk,kb->vacrb/dot_general | solution.py:221
  134.6 2.2 collective-permute-start
  136.8 9.6 %collective-permute-done = bf16[3,4,4096]{2,0,1:T(4,128)(2,1)S(1)} collective-permute-done((bf16[3,4,4096]{2,0,1:T(4,128)(2,1)S(1)}, bf16[3,4,4096]{2,0,1:T(4,128)(2,1)S(1)}, u32[]{:S(2)}, u32[]{:S(2)}) %collective-permute-start) | collective-permute-done | bytes 98336 | tf_op jit(solution)/shard_map/ppermute | solution.py:28
  146.4 64.3 %reduce-scatter.2.cloned.1.call-done = bf16[1,32,4,8,128]{4,3,2,1,0:T(8,128)(2,1)} async-done(((bf16[16,32,4,8,128]{4,3,2,1,0:T(8,128)(2,1)}), bf16[1,32,4,8,128]{4,3,2,1,0:T(8,128)(2,1)}) %reduce-scatter.2.cloned.1.call-update) | async-done | bytes 262160 | tf_op jit(solution)/shard_map/reduce_scatter | solution.py:224
  213.3 1.7 multiply_subtract_fusion
  215.0 4.6 %collective-permute-start.1 = (bf16[3,4,4096]{2,0,1:T(4,128)(2,1)S(1)}, bf16[3,4,4096]{2,0,1:T(4,128)(2,1)S(1)}, u32[]{:S(2)}, u32[]{:S(2)}) collective-permute-start(bf16[3,4,4096]{2,0,1:T(4,128)(2,1)S(1)} %slice.126), channel_id=1, source_target_pairs={{2,0},{4,2},{6,4},{8,6},{10,8},{12,10},{14,12},{16,14},{18,16},{20... | collective-permute-start | bytes 294920 | tf_op jit(solution)/shard_map/ppermute | solution.py:28
  219.6 2.5 %collective-permute-done.1 = bf16[3,4,4096]{2,0,1:T(4,128)(2,1)S(1)} collective-permute-done((bf16[3,4,4096]{2,0,1:T(4,128)(2,1)S(1)}, bf16[3,4,4096]{2,0,1:T(4,128)(2,1)S(1)}, u32[]{:S(2)}, u32[]{:S(2)}) %collective-permute-start.1) | collective-permute-done | bytes 98336 | tf_op jit(solution)/shard_map/ppermute | solution.py:28
  222.2 1.7 multiply_reduce_fusion
  223.9 1.2 collective-permute-start.2
  225.1 1.1 copy.68
  226.2 3.5 %collective-permute-done.2 = bf16[8,4096]{1,0:T(8,128)(2,1)S(1)} collective-permute-done((bf16[8,4096]{1,0:T(8,128)(2,1)S(1)}, bf16[8,4096]{1,0:T(8,128)(2,1)S(1)}, u32[]{:S(2)}, u32[]{:S(2)}) %collective-permute-start.2) | collective-permute-done | bytes 65568 | tf_op jit(solution)/shard_map/ppermute | solution.py:247
  229.8 1.1 copy.69
  (49 shorter events, 13.7 us)
Async XLA Ops:
  7.2 71.6 %all-gather.3.cloned.1.call-start = ((), (), s32[]{:S(2)}) async-start(), calls=%async_computation.2 | async-start | bytes 8912896 | tf_op jit(solution)/shard_map/all_gather | solution.py:189
  14.8 5.4 %copy-start.5 = (bf16[1,1,2,256,128]{4,3,2,1,0:T(8,128)(2,1)S(1)}, bf16[1,1,2,256,128]{4,3,2,1,0:T(8,128)(2,1)}, u32[]{:S(2)}) copy-start(bf16[1,1,2,256,128]{4,3,2,1,0:T(8,128)(2,1)} %param.10) | copy-start | bytes 393220
  20.0 190.7 %reduce-scatter.2.cloned.1.call-start = ((), (), s32[]{:S(2)}) async-start(), calls=%async_computation.1 | async-start | bytes 4456448 | tf_op jit(solution)/shard_map/reduce_scatter | solution.py:224
  20.5 58.2 %copy-start.2 = (bf16[2,256,16,2,8]{1,4,0,3,2:T(8,128)(2,1)}, bf16[2,256,16,2,8]{1,4,0,3,2:T(8,128)(2,1)S(1)}, u32[]{:S(2)}) copy-start(bf16[2,256,16,2,8]{1,4,0,3,2:T(8,128)(2,1)S(1)} %copy.48) | copy-start | bytes 786436
  95.9 2.8 %copy-start.6 = (s32[1,1,16]{2,1,0:T(1,128)S(1)}, s32[1,1,16]{2,1,0:T(1,128)}, u32[]{:S(2)}) copy-start(s32[1,1,16]{2,1,0:T(1,128)} %param.12) | copy-start | bytes 196
  98.6 6.5 %copy-start = (bf16[4,16,16,1,8,128]{5,4,3,2,1,0:T(8,128)(2,1)}, bf16[4,16,16,1,8,128]{5,4,3,2,1,0:T(8,128)(2,1)S(1)}, u32[]{:S(2)}) copy-start(bf16[4,16,16,1,8,128]{5,4,3,2,1,0:T(8,128)(2,1)S(1)} %get-tuple-element.13) | copy-start | bytes 6291460
  124.6 4.1 %copy-start.1 = (bf16[16,32,4,8,128]{4,1,3,0,2:T(8,128)(2,1)S(1)}, bf16[16,32,4,8,128]{4,1,3,0,2:T(8,128)(2,1)}, u32[]{:S(2)}) copy-start(bf16[16,32,4,8,128]{4,1,3,0,2:T(8,128)(2,1)} %get-tuple-element.10) | copy-start | bytes 12582916
  133.2 1.0 copy-start.3
  134.6 11.8 %collective-permute-start = (bf16[3,4,4096]{2,0,1:T(4,128)(2,1)S(1)}, bf16[3,4,4096]{2,0,1:T(4,128)(2,1)S(1)}, u32[]{:S(2)}, u32[]{:S(2)}) collective-permute-start(bf16[3,4,4096]{2,0,1:T(4,128)(2,1)S(1)} %slice.127), channel_id=1, source_target_pairs={{0,2},{2,4},{4,6},{6,8},{8,10},{10,12},{12,14},{14,16},{16,18},{18... | collective-permute-start | bytes 294920 | tf_op jit(solution)/shard_map/ppermute | solution.py:28
  212.4 17.4 %copy-start.4 = (f32[8,4096]{1,0:T(8,128)S(1)}, f32[8,4096]{1,0:T(8,128)}, u32[]{:S(2)}) copy-start(f32[8,4096]{1,0:T(8,128)} %param.9) | copy-start | bytes 393220
  215.0 7.1 %collective-permute-start.1 = (bf16[3,4,4096]{2,0,1:T(4,128)(2,1)S(1)}, bf16[3,4,4096]{2,0,1:T(4,128)(2,1)S(1)}, u32[]{:S(2)}, u32[]{:S(2)}) collective-permute-start(bf16[3,4,4096]{2,0,1:T(4,128)(2,1)S(1)} %slice.126), channel_id=1, source_target_pairs={{2,0},{4,2},{6,4},{8,6},{10,8},{12,10},{14,12},{16,14},{18,16},{20... | collective-permute-start | bytes 294920 | tf_op jit(solution)/shard_map/ppermute | solution.py:28
  223.9 5.9 %collective-permute-start.2 = (bf16[8,4096]{1,0:T(8,128)(2,1)S(1)}, bf16[8,4096]{1,0:T(8,128)(2,1)S(1)}, u32[]{:S(2)}, u32[]{:S(2)}) collective-permute-start(bf16[8,4096]{1,0:T(8,128)(2,1)S(1)} %convert_element_type.114), channel_id=1, source_target_pairs={{0,1},{1,0},{2,3},{3,2},{4,5},{5,4},{6,7},{7,6},{8,9},{9,8},{10,11... | collective-permute-start | bytes 196616 | tf_op jit(solution)/shard_map/ppermute | solution.py:247
Sparse Core Ops, SparseCore 0:
  20.1 58.5 all-gather.2
  133.4 77.2 reduce-scatter.1

commit v5 on v3

--- a/solution.py
+++ b/solution.py
@@ -206,14 +206,12 @@
     tw_s = sin_tw[None, :, None, None, :]
     inv_c = jnp.transpose(cos_sel).astype(bf)
     inv_s = jnp.transpose(sin_sel).astype(bf)
-    part_re = partial[:, :, :, 0]
-    part_im = partial[:, :, :, 1]
-    back_re = jnp.einsum("sa,csvrk->vacrk", inv_c, part_re, preferred_element_type=f32) - jnp.einsum(
-        "sa,csvrk->vacrk", inv_s, part_im, preferred_element_type=f32
-    )
-    back_im = jnp.einsum("sa,csvrk->vacrk", inv_s, part_re, preferred_element_type=f32) + jnp.einsum(
-        "sa,csvrk->vacrk", inv_c, part_im, preferred_element_type=f32
-    )
+    inverse_mat = jnp.stack([jnp.stack([inv_c, -inv_s]), jnp.stack([inv_s, inv_c])])
+    back = jnp.einsum(
+        "jisa,csvirk->jvacrk", inverse_mat, partial, preferred_element_type=f32
+    ).astype(bf)
+    back_re = back[0].astype(f32)
+    back_im = back[1].astype(f32)
     turned_re = (back_re * tw_c - back_im * tw_s).astype(bf)
     turned_im = (back_re * tw_s + back_im * tw_c).astype(bf)
     out_c = (cos_in * unit_scale).astype(bf)

time: 238 us -> 215 us (0.903)
  matrix products: 41.2 us -> 18.1 us
  other arithmetic: 5.08 us -> 8.1 us
  local copies, waits for them, and re-layouts: 14.7 us -> 12 us
    dot_general x4 -> x1, matrix products: 26 us -> 5.54 us  [per_device(): jnp.einsum('jisa,csvirk->jvacrk', inverse_mat, partial, preferred_element...]
    convert_element_type x0 -> x2, other arithmetic: none -> 2.89 us  [the longest x1 2.76 us: per_device(): turned_re = (back_re * tw_c - back_im * tw_s).astype(bf)]
    slice x1 -> x0, local copies, waits for them, and re-layouts: 2.74 us -> none  [per_device(): part_im = partial[:, :, :, 1]]
where the time goes in v5:
time: 215 us
  waiting for transfers between devices  122 us (57%)
  Pallas kernels  31.6 us (15%)
  matrix products  18.1 us (8%)
  between operations  15 us (7%)
  local copies, waits for them, and re-layouts  12 us (6%)
  other arithmetic  8.1 us (4%)
  starting transfers between devices  8.04 us (4%)
    all_gather x1, waiting for transfers between devices, per_device(): gathered = lax.all_gather(panel_t, 'vis', axis=0)  56.3 us
    reduce_scatter x1, waiting for transfers between devices, per_device(): lax.psum_scatter(rows_part.astype(bf), 'vis', scatter_dimension=0, tiled=...  51.5 us
    pallas_call x1, Pallas kernels, degrid_grid(): pl.pallas_call(degrid_body, grid_spec=pltpu.PrefetchScalarGridSpec(num_sc...  31.6 us
    ppermute x2, waiting for transfers between devices, shifted(): lax.ppermute(value, axis, [(source, source + steps) for source in range(i...  10.9 us
    ppermute x2, starting transfers between devices, shifted(): lax.ppermute(value, axis, [(source, source + steps) for source in range(i...  6.57 us
    dot_general x1, matrix products, per_device(): jnp.einsum('jisa,csvirk->jvacrk', inverse_mat, partial, preferred_element...  5.54 us
    dot_general x4, matrix products, along_inner(): jnp.einsum('qkb,bj->qkj', values, table, precision=highest, preferred_ele...  4.31 us
  transfers between devices with their start and end apart: 5, of which 5 were waited for; matrix products, arithmetic and copies ran while one was open for 1% of the time, Pallas kernels for 0%

profile of v5, /device:TPU:24, one launch (start us, length us, event | category | flops | bytes accessed | tf_op | source)
XLA Modules:
  0.0 215.1 jit_solution(15782286947896504274)
XLA Ops:
  7.7 1.4 reshape_reshape.3
  11.0 1.1 fusion.48
  12.1 1.1 fusion.44
  13.2 1.1 fusion.21
  15.9 1.1 fusion.20
  17.5 1.0 mul.485
  18.9 1.1 copy.55
  22.4 56.3 %all-gather.3.cloned.1.call-done = bf16[64,2,8,4096]{3,2,1,0:T(8,128)(2,1)} async-done(((bf16[4,2,8,4096]{3,2,1,0:T(8,128)(2,1)}), bf16[64,2,8,4096]{3,2,1,0:T(8,128)(2,1)}) %all-gather.3.cloned.1.call-update) | async-done | bytes 8388624 | tf_op jit(solution)/shard_map/all_gather | solution.py:189
  78.8 31.6 %shard_map.86 = bf16[4,16,256,128]{3,2,1,0:T(8,128)(2,1)} custom-call(s32[16]{0:T(128)} %bitcast.111, s32[1]{0:T(128)} %bitcast.100.count_ref, bf16[512,256]{1,0:T(8,128)(2,1)} %copy.56.kmat_ref, bf16[256,512]{1,0:T(8,128)(2,1)} %bitcast.108, bf16[16,4,2,8,4096]{4,3,2,1,0:T(8,128)(2,1)} %bitcast.101, bf16[16,4,2,8,4096]{4,3,2,1,0:T(8,128)(2,1)} %bitcast.102, ...), custom_call_target="tpu_custom_call" | custom-call | flops 4294967296 | bytes 16777216 | tf_op jit(solution)/shard_map/pallas_call | solution.py:145
  110.4 5.5 %fusion.4 = bf16[2,16,32,4,8,128]{5,2,0,4,1,3:T(8,128)(2,1)S(1)} fusion(bf16[4,16,16,2,8,128,1]{5,4,3,2,1,0,6:T(8,128)(2,1)} %bitcast.105, bf16[1,2,16,32]{3,2,1,0:T(8,128)(2,1)S(1)} %get-tuple-element.17, bf16[1,2,16,32]{3,2,1,0:T(8,128)(2,1)S(1)} %get-tuple-element.16), kind=kOutput, calls=%fused_computation.10 | convolution fusion | flops 272637952 | bytes 12587008 | tf_op jit(solution)/shard_map/jisa,csvirk->jvacrk/dot_general | solution.py:210
  116.0 2.8 %fusion.1 = (bf16[16,32,4,8,128]{4,1,3,0,2:T(8,128)(2,1)S(1)}, bf16[16,32,4,8,128]{4,1,3,0,2:T(8,128)(2,1)S(1)}) fusion(f32[32,128]{1,0:T(8,128)S(1)} %fusion.101, f32[32,128]{1,0:T(8,128)S(1)} %get-tuple-element.21, bf16[2,16,32,4,8,128]{5,2,0,4,1,3:T(8,128)(2,1)S(1)} %fusion.4), kind=kLoop, calls=%fused_computation.6 | loop fusion | flops 20971520 | bytes 16809984 | tf_op jit(solution)/shard_map/convert_element_type | solution.py:215
  118.7 1.8 fusion.6
  120.5 4.2 %subtract_convert_fusion = bf16[16,32,4,8,128]{4,3,2,1,0:T(8,128)(2,1)} fusion(f32[16,32,4,8,128]{4,3,2,1,0:T(8,128)S(1)} %fusion.6, bf16[16,32,4,8,128]{4,1,3,0,2:T(8,128)(2,1)S(1)} %get-tuple-element.10), kind=kOutput, calls=%fused_computation.9 | convolution fusion | flops 541327360 | bytes 16777216 | tf_op jit(solution)/shard_map/vacrk,kb->vacrb/dot_general | solution.py:219
  126.1 2.1 collective-permute-start
  128.3 8.4 %collective-permute-done = bf16[3,4,4096]{2,0,1:T(4,128)(2,1)S(1)} collective-permute-done((bf16[3,4,4096]{2,0,1:T(4,128)(2,1)S(1)}, bf16[3,4,4096]{2,0,1:T(4,128)(2,1)S(1)}, u32[]{:S(2)}, u32[]{:S(2)}) %collective-permute-start) | collective-permute-done | bytes 98336 | tf_op jit(solution)/shard_map/ppermute | solution.py:28
  136.7 51.5 %reduce-scatter.2.cloned.1.call-done = bf16[1,32,4,8,128]{4,3,2,1,0:T(8,128)(2,1)} async-done(((bf16[16,32,4,8,128]{4,3,2,1,0:T(8,128)(2,1)}), bf16[1,32,4,8,128]{4,3,2,1,0:T(8,128)(2,1)}) %reduce-scatter.2.cloned.1.call-update) | async-done | bytes 262160 | tf_op jit(solution)/shard_map/reduce_scatter | solution.py:222
  190.8 1.7 multiply_subtract_fusion
  192.5 4.4 %collective-permute-start.1 = (bf16[3,4,4096]{2,0,1:T(4,128)(2,1)S(1)}, bf16[3,4,4096]{2,0,1:T(4,128)(2,1)S(1)}, u32[]{:S(2)}, u32[]{:S(2)}) collective-permute-start(bf16[3,4,4096]{2,0,1:T(4,128)(2,1)S(1)} %slice.136), channel_id=1, source_target_pairs={{2,0},{4,2},{6,4},{8,6},{10,8},{12,10},{14,12},{16,14},{18,16},{20... | collective-permute-start | bytes 294920 | tf_op jit(solution)/shard_map/ppermute | solution.py:28
  196.9 2.5 %collective-permute-done.1 = bf16[3,4,4096]{2,0,1:T(4,128)(2,1)S(1)} collective-permute-done((bf16[3,4,4096]{2,0,1:T(4,128)(2,1)S(1)}, bf16[3,4,4096]{2,0,1:T(4,128)(2,1)S(1)}, u32[]{:S(2)}, u32[]{:S(2)}) %collective-permute-start.1) | collective-permute-done | bytes 98336 | tf_op jit(solution)/shard_map/ppermute | solution.py:28
  199.5 1.7 multiply_reduce_fusion
  201.2 1.2 collective-permute-start.2
  202.4 1.1 copy.68
  203.5 3.5 %collective-permute-done.2 = bf16[8,4096]{1,0:T(8,128)(2,1)S(1)} collective-permute-done((bf16[8,4096]{1,0:T(8,128)(2,1)S(1)}, bf16[8,4096]{1,0:T(8,128)(2,1)S(1)}, u32[]{:S(2)}, u32[]{:S(2)}) %collective-permute-start.2) | collective-permute-done | bytes 65568 | tf_op jit(solution)/shard_map/ppermute | solution.py:245
  207.1 1.1 copy.69
  (45 shorter events, 10.8 us)
Async XLA Ops:
  7.2 71.6 %all-gather.3.cloned.1.call-start = ((), (), s32[]{:S(2)}) async-start(), calls=%async_computation.2 | async-start | bytes 8912896 | tf_op jit(solution)/shard_map/all_gather | solution.py:189
  14.8 5.4 %copy-start.3 = (bf16[1,1,2,256,128]{4,3,2,1,0:T(8,128)(2,1)S(1)}, bf16[1,1,2,256,128]{4,3,2,1,0:T(8,128)(2,1)}, u32[]{:S(2)}) copy-start(bf16[1,1,2,256,128]{4,3,2,1,0:T(8,128)(2,1)} %param.10) | copy-start | bytes 393220
  15.9 6.3 %copy-start.4 = (s32[1,1,16]{2,1,0:T(1,128)S(1)}, s32[1,1,16]{2,1,0:T(1,128)}, u32[]{:S(2)}) copy-start(s32[1,1,16]{2,1,0:T(1,128)} %param.12) | copy-start | bytes 196
  20.0 168.2 %reduce-scatter.2.cloned.1.call-start = ((), (), s32[]{:S(2)}) async-start(), calls=%async_computation.1 | async-start | bytes 4456448 | tf_op jit(solution)/shard_map/reduce_scatter | solution.py:222
  20.6 58.2 %copy-start = (bf16[2,256,16,2,8]{1,4,0,3,2:T(8,128)(2,1)}, bf16[2,256,16,2,8]{1,4,0,3,2:T(8,128)(2,1)S(1)}, u32[]{:S(2)}) copy-start(bf16[2,256,16,2,8]{1,4,0,3,2:T(8,128)(2,1)S(1)} %copy.48) | copy-start | bytes 786436
  124.7 1.0 copy-start.1
  126.1 10.5 %collective-permute-start = (bf16[3,4,4096]{2,0,1:T(4,128)(2,1)S(1)}, bf16[3,4,4096]{2,0,1:T(4,128)(2,1)S(1)}, u32[]{:S(2)}, u32[]{:S(2)}) collective-permute-start(bf16[3,4,4096]{2,0,1:T(4,128)(2,1)S(1)} %slice.137), channel_id=1, source_target_pairs={{0,2},{2,4},{4,6},{6,8},{8,10},{10,12},{12,14},{14,16},{16,18},{18... | collective-permute-start | bytes 294920 | tf_op jit(solution)/shard_map/ppermute | solution.py:28
  189.8 17.2 %copy-start.2 = (f32[8,4096]{1,0:T(8,128)S(1)}, f32[8,4096]{1,0:T(8,128)}, u32[]{:S(2)}) copy-start(f32[8,4096]{1,0:T(8,128)} %param.9) | copy-start | bytes 393220
  192.5 6.9 %collective-permute-start.1 = (bf16[3,4,4096]{2,0,1:T(4,128)(2,1)S(1)}, bf16[3,4,4096]{2,0,1:T(4,128)(2,1)S(1)}, u32[]{:S(2)}, u32[]{:S(2)}) collective-permute-start(bf16[3,4,4096]{2,0,1:T(4,128)(2,1)S(1)} %slice.136), channel_id=1, source_target_pairs={{2,0},{4,2},{6,4},{8,6},{10,8},{12,10},{14,12},{16,14},{18,16},{20... | collective-permute-start | bytes 294920 | tf_op jit(solution)/shard_map/ppermute | solution.py:28
  201.2 5.9 %collective-permute-start.2 = (bf16[8,4096]{1,0:T(8,128)(2,1)S(1)}, bf16[8,4096]{1,0:T(8,128)(2,1)S(1)}, u32[]{:S(2)}, u32[]{:S(2)}) collective-permute-start(bf16[8,4096]{1,0:T(8,128)(2,1)S(1)} %convert_element_type.171), channel_id=1, source_target_pairs={{0,1},{1,0},{2,3},{3,2},{4,5},{5,4},{6,7},{7,6},{8,9},{9,8},{10,11... | collective-permute-start | bytes 196616 | tf_op jit(solution)/shard_map/ppermute | solution.py:245
Sparse Core Ops, SparseCore 0:
  20.1 58.5 all-gather.2
  124.9 63.2 reduce-scatter.1

commit v6 on v5

--- a/solution.py
+++ b/solution.py
@@ -212,14 +212,14 @@
     ).astype(bf)
     back_re = back[0].astype(f32)
     back_im = back[1].astype(f32)
-    turned_re = (back_re * tw_c - back_im * tw_s).astype(bf)
-    turned_im = (back_re * tw_s + back_im * tw_c).astype(bf)
-    out_c = (cos_in * unit_scale).astype(bf)
-    out_s = (sin_in * unit_scale).astype(bf)
-    rows_part = jnp.einsum("vacrk,kb->vacrb", turned_re, out_c, preferred_element_type=f32) - jnp.einsum(
-        "vacrk,kb->vacrb", turned_im, out_s, preferred_element_type=f32
-    )
-    rows_sum = lax.psum_scatter(rows_part.astype(bf), "vis", scatter_dimension=0, tiled=True)
+    turned = jnp.stack(
+        [back_re * tw_c - back_im * tw_s, back_re * tw_s + back_im * tw_c]
+    ).astype(bf)
+    out_table = jnp.stack([cos_in * unit_scale, -sin_in * unit_scale]).astype(bf)
+    rows_part = jnp.einsum(
+        "jvacrk,jkb->vacrb", turned, out_table, preferred_element_type=f32
+    ).astype(bf)
+    rows_sum = lax.psum_scatter(rows_part, "vis", scatter_dimension=0, tiled=True)
     gradient = (
         jnp.transpose(rows_sum[0].astype(f32), (2, 1, 3, 0))
         .reshape(panel_rows, chan_count, grid_width)

time: 215 us -> 228 us (1.060)
  other arithmetic: 8.1 us -> 16.2 us
  waiting for transfers between devices: 122 us -> 128 us
  Pallas kernels: 31.6 us -> 25.8 us
  matrix products: 18.1 us -> 22.9 us
    another operation x0 -> x3, other arithmetic: none -> 10.9 us  [the longest x1 6.49 us: per_device(): jnp.stack([back_re * tw_c - back_im * tw_s, back_re * tw_s + back_im * tw...]
    pallas_call x1, Pallas kernels: 31.6 us -> 25.8 us  [degrid_grid(): pl.pallas_call(degrid_body, grid_spec=pltpu.PrefetchScalarGridSpec(num_sc...]
    reduce_scatter x1, waiting for transfers between devices: 51.5 us -> 57.2 us  [per_device(): lax.psum_scatter(rows_part, 'vis', scatter_dimension=0, tiled=True)]
    dot_general x2 -> x1, matrix products: 6 us -> 10.7 us  [per_device(): jnp.einsum('jvacrk,jkb->vacrb', turned, out_table, preferred_element_type...]
    convert_element_type x1 -> x0, other arithmetic: 2.76 us -> none  [per_device(): turned_re = (back_re * tw_c - back_im * tw_s).astype(bf)]
where the time goes in v6:
time: 228 us; the launch traced here: 227 us
  waiting for transfers between devices  128 us (56%)
  Pallas kernels  25.8 us (11%)
  matrix products  22.9 us (10%)
  other arithmetic  16.2 us (7%)
  between operations  15 us (7%)
  local copies, waits for them, and re-layouts  11 us (5%)
  starting transfers between devices  7.92 us (3%)
    reduce_scatter x1, waiting for transfers between devices, per_device(): lax.psum_scatter(rows_part, 'vis', scatter_dimension=0, tiled=True)  57.2 us
    all_gather x1, waiting for transfers between devices, per_device(): gathered = lax.all_gather(panel_t, 'vis', axis=0)  56 us
    pallas_call x1, Pallas kernels, degrid_grid(): pl.pallas_call(degrid_body, grid_spec=pltpu.PrefetchScalarGridSpec(num_sc...  25.8 us
    ppermute x2, waiting for transfers between devices, shifted(): lax.ppermute(value, axis, [(source, source + steps) for source in range(i...  11.1 us
    dot_general x1, matrix products, per_device(): jnp.einsum('jvacrk,jkb->vacrb', turned, out_table, preferred_element_type...  10.7 us
    ppermute x2, starting transfers between devices, shifted(): lax.ppermute(value, axis, [(source, source + steps) for source in range(i...  6.53 us
    another operation x1, other arithmetic, per_device(): jnp.stack([back_re * tw_c - back_im * tw_s, back_re * tw_s + back_im * tw...  6.49 us
    dot_general x1, matrix products, per_device(): jnp.einsum('jisa,csvirk->jvacrk', inverse_mat, partial, preferred_element...  5.54 us
  transfers between devices with their start and end apart: 5, of which 5 were waited for; matrix products, arithmetic and copies ran while one was open for 1% of the time, Pallas kernels for 0%

profile of v6, /device:TPU:24, one launch (start us, length us, event | category | flops | bytes accessed | tf_op | source)
XLA Modules:
  0.0 226.7 jit_solution(5939360939936397442)
XLA Ops:
  7.7 1.4 reshape_reshape.3
  11.1 1.1 fusion.46
  12.1 1.1 fusion.42
  13.2 1.1 fusion.19
  14.8 1.0 mul.521
  15.9 1.1 fusion.18
  18.9 1.1 copy.51
  22.7 56.0 %all-gather.3.cloned.1.call-done = bf16[64,2,8,4096]{3,2,1,0:T(8,128)(2,1)} async-done(((bf16[4,2,8,4096]{3,2,1,0:T(8,128)(2,1)}), bf16[64,2,8,4096]{3,2,1,0:T(8,128)(2,1)}) %all-gather.3.cloned.1.call-update) | async-done | bytes 8388624 | tf_op jit(solution)/shard_map/all_gather | solution.py:189
  78.8 25.8 %shard_map.86 = bf16[4,16,256,128]{3,2,1,0:T(8,128)(2,1)} custom-call(s32[16]{0:T(128)} %bitcast.93, s32[1]{0:T(128)} %bitcast.82.count_ref, bf16[512,256]{1,0:T(8,128)(2,1)} %copy.52.kmat_ref, bf16[256,512]{1,0:T(8,128)(2,1)} %bitcast.90, bf16[16,4,2,8,4096]{4,3,2,1,0:T(8,128)(2,1)} %bitcast.83, bf16[16,4,2,8,4096]{4,3,2,1,0:T(8,128)(2,1)} %bitcast.84, ...), custom_call_target="tpu_custom_call" | custom-call | flops 4294967296 | bytes 16777216 | tf_op jit(solution)/shard_map/pallas_call | solution.py:145
  104.6 5.5 %fusion.6 = bf16[2,16,32,4,8,128]{5,2,0,4,1,3:T(8,128)(2,1)S(1)} fusion(bf16[4,16,16,2,8,128,1]{5,4,3,2,1,0,6:T(8,128)(2,1)} %bitcast.87, bf16[1,2,16,32]{3,2,1,0:T(8,128)(2,1)S(1)} %get-tuple-element.17, bf16[1,2,16,32]{3,2,1,0:T(8,128)(2,1)S(1)} %get-tuple-element.16), kind=kOutput, calls=%fused_computation.13 | convolution fusion | flops 272637952 | bytes 12587008 | tf_op jit(solution)/shard_map/jisa,csvirk->jvacrk/dot_general | solution.py:210
  110.1 4.1 %fusion.1 = (bf16[1,16,32,4,8,128]{5,2,0,4,1,3:T(8,128)(2,1)S(1)}, bf16[1,16,32,4,8,128]{5,2,0,4,1,3:T(8,128)(2,1)}) fusion(f32[32,128]{1,0:T(8,128)S(1)} %fusion.99, f32[32,128]{1,0:T(8,128)S(1)} %get-tuple-element.21, bf16[2,16,32,4,8,128]{5,2,0,4,1,3:T(8,128)(2,1)S(1)} %fusion.6), kind=kLoop, calls=%fused_computation.6 | loop fusion | flops 20971520 | bytes 16809984 | tf_op jit(solution)/shard_map/convert.7
  114.3 6.5 %pad_maximum_fusion = bf16[2,16,32,4,8,128]{5,2,0,4,1,3:T(8,128)(2,1)} fusion(bf16[1,16,32,4,8,128]{5,2,0,4,1,3:T(8,128)(2,1)} %get-tuple-element.11, bf16[1,16,32,4,8,128]{5,2,0,4,1,3:T(8,128)(2,1)S(1)} %get-tuple-element.10), kind=kLoop, calls=%fused_computation.9 | loop fusion | flops 4194304 | bytes 16777216 | tf_op jit(solution)/shard_map/stack | solution.py:215
  120.8 10.7 %bitcast_convert_fusion.1 = bf16[16,32,4,8,128]{4,3,2,1,0:T(8,128)(2,1)} fusion(bf16[2,16,32,4,8,128]{5,2,0,4,1,3:T(8,128)(2,1)} %pad_maximum_fusion, bf16[1,128,128]{2,1,0:T(8,128)(2,1)S(1)} %get-tuple-element.22, bf16[1,128,128]{2,1,0:T(8,128)(2,1)S(1)} %get-tuple-element.23), kind=kOutput, calls=%fused_computation.10 | convolution fusion | flops 1075871744 | bytes 12648448 | tf_op jit(solution)/shard_map/jvacrk,jkb->vacrb/dot_general | solution.py:219
  131.9 1.9 collective-permute-start
  133.8 8.6 %collective-permute-done = bf16[3,4,4096]{2,0,1:T(4,128)(2,1)S(1)} collective-permute-done((bf16[3,4,4096]{2,0,1:T(4,128)(2,1)S(1)}, bf16[3,4,4096]{2,0,1:T(4,128)(2,1)S(1)}, u32[]{:S(2)}, u32[]{:S(2)}) %collective-permute-start) | collective-permute-done | bytes 98336 | tf_op jit(solution)/shard_map/ppermute | solution.py:28
  142.4 57.2 %reduce-scatter.2.cloned.1.call-done = bf16[1,32,4,8,128]{4,3,2,1,0:T(8,128)(2,1)} async-done(((bf16[16,32,4,8,128]{4,3,2,1,0:T(8,128)(2,1)}), bf16[1,32,4,8,128]{4,3,2,1,0:T(8,128)(2,1)}) %reduce-scatter.2.cloned.1.call-update) | async-done | bytes 262160 | tf_op jit(solution)/shard_map/reduce_scatter | solution.py:222
  202.2 1.7 multiply_subtract_fusion
  203.9 4.6 %collective-permute-start.1 = (bf16[3,4,4096]{2,0,1:T(4,128)(2,1)S(1)}, bf16[3,4,4096]{2,0,1:T(4,128)(2,1)S(1)}, u32[]{:S(2)}, u32[]{:S(2)}) collective-permute-start(bf16[3,4,4096]{2,0,1:T(4,128)(2,1)S(1)} %slice.130), channel_id=1, source_target_pairs={{2,0},{4,2},{6,4},{8,6},{10,8},{12,10},{14,12},{16,14},{18,16},{20... | collective-permute-start | bytes 294920 | tf_op jit(solution)/shard_map/ppermute | solution.py:28
  208.6 2.5 %collective-permute-done.1 = bf16[3,4,4096]{2,0,1:T(4,128)(2,1)S(1)} collective-permute-done((bf16[3,4,4096]{2,0,1:T(4,128)(2,1)S(1)}, bf16[3,4,4096]{2,0,1:T(4,128)(2,1)S(1)}, u32[]{:S(2)}, u32[]{:S(2)}) %collective-permute-start.1) | collective-permute-done | bytes 98336 | tf_op jit(solution)/shard_map/ppermute | solution.py:28
  211.1 1.7 multiply_reduce_fusion
  212.8 1.1 collective-permute-start.2
  213.9 1.1 copy.62
  215.0 3.6 %collective-permute-done.2 = bf16[8,4096]{1,0:T(8,128)(2,1)S(1)} collective-permute-done((bf16[8,4096]{1,0:T(8,128)(2,1)S(1)}, bf16[8,4096]{1,0:T(8,128)(2,1)S(1)}, u32[]{:S(2)}, u32[]{:S(2)}) %collective-permute-start.2) | collective-permute-done | bytes 65568 | tf_op jit(solution)/shard_map/ppermute | solution.py:245
  218.8 1.1 copy.63
  (46 shorter events, 10.1 us)
Async XLA Ops:
  7.2 71.6 %all-gather.3.cloned.1.call-start = ((), (), s32[]{:S(2)}) async-start(), calls=%async_computation.2 | async-start | bytes 8912896 | tf_op jit(solution)/shard_map/all_gather | solution.py:189
  9.8 10.4 %copy-start.3 = (bf16[1,1,2,256,128]{4,3,2,1,0:T(8,128)(2,1)S(1)}, bf16[1,1,2,256,128]{4,3,2,1,0:T(8,128)(2,1)}, u32[]{:S(2)}) copy-start(bf16[1,1,2,256,128]{4,3,2,1,0:T(8,128)(2,1)} %param.10) | copy-start | bytes 393220
  10.3 11.9 %copy-start.4 = (s32[1,1,16]{2,1,0:T(1,128)S(1)}, s32[1,1,16]{2,1,0:T(1,128)}, u32[]{:S(2)}) copy-start(s32[1,1,16]{2,1,0:T(1,128)} %param.12) | copy-start | bytes 196
  20.0 179.6 %reduce-scatter.2.cloned.1.call-start = ((), (), s32[]{:S(2)}) async-start(), calls=%async_computation.1 | async-start | bytes 4456448 | tf_op jit(solution)/shard_map/reduce_scatter | solution.py:222
  20.6 58.2 %copy-start = (bf16[2,256,16,2,8]{1,4,0,3,2:T(8,128)(2,1)}, bf16[2,256,16,2,8]{1,4,0,3,2:T(8,128)(2,1)S(1)}, u32[]{:S(2)}) copy-start(bf16[2,256,16,2,8]{1,4,0,3,2:T(8,128)(2,1)S(1)} %copy.44) | copy-start | bytes 786436
  120.7 10.7 %copy-start.1 = (f32[8,4,4096]{2,1,0:T(4,128)S(1)}, f32[8,4,4096]{2,1,0:T(4,128)}, u32[]{:S(2)}) copy-start(f32[8,4,4096]{2,1,0:T(4,128)} %param.8) | copy-start | bytes 1572868
  131.5 87.2 %copy-start.2 = (f32[8,4096]{1,0:T(8,128)S(1)}, f32[8,4096]{1,0:T(8,128)}, u32[]{:S(2)}) copy-start(f32[8,4096]{1,0:T(8,128)} %param.9) | copy-start | bytes 393220
  131.9 10.5 %collective-permute-start = (bf16[3,4,4096]{2,0,1:T(4,128)(2,1)S(1)}, bf16[3,4,4096]{2,0,1:T(4,128)(2,1)S(1)}, u32[]{:S(2)}, u32[]{:S(2)}) collective-permute-start(bf16[3,4,4096]{2,0,1:T(4,128)(2,1)S(1)} %slice.131), channel_id=1, source_target_pairs={{0,2},{2,4},{4,6},{6,8},{8,10},{10,12},{12,14},{14,16},{16,18},{18... | collective-permute-start | bytes 294920 | tf_op jit(solution)/shard_map/ppermute | solution.py:28
  203.9 7.1 %collective-permute-start.1 = (bf16[3,4,4096]{2,0,1:T(4,128)(2,1)S(1)}, bf16[3,4,4096]{2,0,1:T(4,128)(2,1)S(1)}, u32[]{:S(2)}, u32[]{:S(2)}) collective-permute-start(bf16[3,4,4096]{2,0,1:T(4,128)(2,1)S(1)} %slice.130), channel_id=1, source_target_pairs={{2,0},{4,2},{6,4},{8,6},{10,8},{12,10},{14,12},{16,14},{18,16},{20... | collective-permute-start | bytes 294920 | tf_op jit(solution)/shard_map/ppermute | solution.py:28
  212.8 5.9 %collective-permute-start.2 = (bf16[8,4096]{1,0:T(8,128)(2,1)S(1)}, bf16[8,4096]{1,0:T(8,128)(2,1)S(1)}, u32[]{:S(2)}, u32[]{:S(2)}) collective-permute-start(bf16[8,4096]{1,0:T(8,128)(2,1)S(1)} %convert_element_type.165), channel_id=1, source_target_pairs={{0,1},{1,0},{2,3},{3,2},{4,5},{5,4},{6,7},{7,6},{8,9},{9,8},{10,11... | collective-permute-start | bytes 196616 | tf_op jit(solution)/shard_map/ppermute | solution.py:245
Sparse Core Ops, SparseCore 0:
  20.1 58.5 all-gather.2
  131.6 67.9 reduce-scatter.1

commit v7 on v5

--- a/solution.py
+++ b/solution.py
@@ -19,7 +19,7 @@
 primal_step = 0.2
 dual_step = 0.5
 tile_width = 128
-highest = lax.Precision.HIGHEST
+highest = lax.Precision.HIGH
 
 
 def shifted(value, axis, steps):

time: 215 us -> 214 us (level)
  Pallas kernels: 31.6 us -> 25.8 us
  starting transfers between devices: 8.04 us -> 11.9 us
    pallas_call x1, Pallas kernels: 31.6 us -> 25.8 us  [degrid_grid(): pl.pallas_call(degrid_body, grid_spec=pltpu.PrefetchScalarGridSpec(num_sc...]
    ppermute x2, starting transfers between devices: 6.57 us -> 10.3 us  [shifted(): lax.ppermute(value, axis, [(source, source + steps) for source in range(i...]
where the time goes in v7:
time: 214 us; the launch traced here: 212 us
  waiting for transfers between devices  123 us (57%)
  Pallas kernels  25.8 us (12%)
  matrix products  16.5 us (8%)
  between operations  15 us (7%)
  local copies, waits for them, and re-layouts  12 us (6%)
  starting transfers between devices  11.9 us (6%)
  other arithmetic  8.1 us (4%)
    all_gather x1, waiting for transfers between devices, per_device(): gathered = lax.all_gather(panel_t, 'vis', axis=0)  56.3 us
    reduce_scatter x1, waiting for transfers between devices, per_device(): lax.psum_scatter(rows_part.astype(bf), 'vis', scatter_dimension=0, tiled=...  50.9 us
    pallas_call x1, Pallas kernels, degrid_grid(): pl.pallas_call(degrid_body, grid_spec=pltpu.PrefetchScalarGridSpec(num_sc...  25.8 us
    ppermute x2, waiting for transfers between devices, shifted(): lax.ppermute(value, axis, [(source, source + steps) for source in range(i...  12.4 us
    ppermute x2, starting transfers between devices, shifted(): lax.ppermute(value, axis, [(source, source + steps) for source in range(i...  10.3 us
    dot_general x1, matrix products, per_device(): jnp.einsum('jisa,csvirk->jvacrk', inverse_mat, partial, preferred_element...  5.54 us
  transfers between devices with their start and end apart: 5, of which 5 were waited for; matrix products, arithmetic and copies ran while one was open for 1% of the time, Pallas kernels for 0%

profile of v7, /device:TPU:24, one launch (start us, length us, event | category | flops | bytes accessed | tf_op | source)
XLA Modules:
  0.0 212.4 jit_solution(7192185139628235530)
XLA Ops:
  7.6 1.4 reshape_reshape.3
  13.4 1.0 mul.481
  15.9 1.0 mul.485
  17.3 1.1 copy.55
  20.8 56.3 %all-gather.3.cloned.1.call-done = bf16[64,2,8,4096]{3,2,1,0:T(8,128)(2,1)} async-done(((bf16[4,2,8,4096]{3,2,1,0:T(8,128)(2,1)}), bf16[64,2,8,4096]{3,2,1,0:T(8,128)(2,1)}) %all-gather.3.cloned.1.call-update) | async-done | bytes 8388624 | tf_op jit(solution)/shard_map/all_gather | solution.py:189
  77.2 25.8 %shard_map.86 = bf16[4,16,256,128]{3,2,1,0:T(8,128)(2,1)} custom-call(s32[16]{0:T(128)} %bitcast.111, s32[1]{0:T(128)} %bitcast.100.count_ref, bf16[512,256]{1,0:T(8,128)(2,1)} %copy.56.kmat_ref, bf16[256,512]{1,0:T(8,128)(2,1)} %bitcast.108, bf16[16,4,2,8,4096]{4,3,2,1,0:T(8,128)(2,1)} %bitcast.101, bf16[16,4,2,8,4096]{4,3,2,1,0:T(8,128)(2,1)} %bitcast.102, ...), custom_call_target="tpu_custom_call" | custom-call | flops 4294967296 | bytes 16777216 | tf_op jit(solution)/shard_map/pallas_call | solution.py:145
  103.0 5.5 %fusion.4 = bf16[2,16,32,4,8,128]{5,2,0,4,1,3:T(8,128)(2,1)S(1)} fusion(bf16[4,16,16,2,8,128,1]{5,4,3,2,1,0,6:T(8,128)(2,1)} %bitcast.105, bf16[1,2,16,32]{3,2,1,0:T(8,128)(2,1)S(1)} %get-tuple-element.17, bf16[1,2,16,32]{3,2,1,0:T(8,128)(2,1)S(1)} %get-tuple-element.16), kind=kOutput, calls=%fused_computation.10 | convolution fusion | flops 272637952 | bytes 12587008 | tf_op jit(solution)/shard_map/jisa,csvirk->jvacrk/dot_general | solution.py:210
  108.5 2.8 %fusion.1 = (bf16[16,32,4,8,128]{4,1,3,0,2:T(8,128)(2,1)S(1)}, bf16[16,32,4,8,128]{4,1,3,0,2:T(8,128)(2,1)S(1)}) fusion(f32[32,128]{1,0:T(8,128)S(1)} %fusion.101, f32[32,128]{1,0:T(8,128)S(1)} %get-tuple-element.21, bf16[2,16,32,4,8,128]{5,2,0,4,1,3:T(8,128)(2,1)S(1)} %fusion.4), kind=kLoop, calls=%fused_computation.6 | loop fusion | flops 20971520 | bytes 16809984 | tf_op jit(solution)/shard_map/convert_element_type | solution.py:215
  111.3 1.8 fusion.6
  113.1 4.2 %subtract_convert_fusion = bf16[16,32,4,8,128]{4,3,2,1,0:T(8,128)(2,1)} fusion(f32[16,32,4,8,128]{4,3,2,1,0:T(8,128)S(1)} %fusion.6, bf16[16,32,4,8,128]{4,1,3,0,2:T(8,128)(2,1)S(1)} %get-tuple-element.10), kind=kOutput, calls=%fused_computation.9 | convolution fusion | flops 541327360 | bytes 16777216 | tf_op jit(solution)/shard_map/vacrk,kb->vacrb/dot_general | solution.py:219
  117.3 1.0 copy-done.1
  118.7 5.8 %collective-permute-start = (bf16[3,4,4096]{2,0,1:T(4,128)(2,1)S(1)}, bf16[3,4,4096]{2,0,1:T(4,128)(2,1)S(1)}, u32[]{:S(2)}, u32[]{:S(2)}) collective-permute-start(bf16[3,4,4096]{2,0,1:T(4,128)(2,1)S(1)} %slice.137), channel_id=1, source_target_pairs={{0,2},{2,4},{4,6},{6,8},{8,10},{10,12},{12,14},{14,16},{16,18},{18... | collective-permute-start | bytes 294920 | tf_op jit(solution)/shard_map/ppermute | solution.py:28
  124.5 9.9 %collective-permute-done = bf16[3,4,4096]{2,0,1:T(4,128)(2,1)S(1)} collective-permute-done((bf16[3,4,4096]{2,0,1:T(4,128)(2,1)S(1)}, bf16[3,4,4096]{2,0,1:T(4,128)(2,1)S(1)}, u32[]{:S(2)}, u32[]{:S(2)}) %collective-permute-start) | collective-permute-done | bytes 98336 | tf_op jit(solution)/shard_map/ppermute | solution.py:28
  134.5 50.9 %reduce-scatter.2.cloned.1.call-done = bf16[1,32,4,8,128]{4,3,2,1,0:T(8,128)(2,1)} async-done(((bf16[16,32,4,8,128]{4,3,2,1,0:T(8,128)(2,1)}), bf16[1,32,4,8,128]{4,3,2,1,0:T(8,128)(2,1)}) %reduce-scatter.2.cloned.1.call-update) | async-done | bytes 262160 | tf_op jit(solution)/shard_map/reduce_scatter | solution.py:222
  185.4 1.0 convert_bitcast_fusion
  187.0 1.0 reshape.325
  188.0 1.7 multiply_subtract_fusion
  189.7 4.5 %collective-permute-start.1 = (bf16[3,4,4096]{2,0,1:T(4,128)(2,1)S(1)}, bf16[3,4,4096]{2,0,1:T(4,128)(2,1)S(1)}, u32[]{:S(2)}, u32[]{:S(2)}) collective-permute-start(bf16[3,4,4096]{2,0,1:T(4,128)(2,1)S(1)} %slice.136), channel_id=1, source_target_pairs={{2,0},{4,2},{6,4},{8,6},{10,8},{12,10},{14,12},{16,14},{18,16},{20... | collective-permute-start | bytes 294920 | tf_op jit(solution)/shard_map/ppermute | solution.py:28
  194.2 2.5 %collective-permute-done.1 = bf16[3,4,4096]{2,0,1:T(4,128)(2,1)S(1)} collective-permute-done((bf16[3,4,4096]{2,0,1:T(4,128)(2,1)S(1)}, bf16[3,4,4096]{2,0,1:T(4,128)(2,1)S(1)}, u32[]{:S(2)}, u32[]{:S(2)}) %collective-permute-start.1) | collective-permute-done | bytes 98336 | tf_op jit(solution)/shard_map/ppermute | solution.py:28
  196.7 1.7 multiply_reduce_fusion
  198.4 1.3 collective-permute-start.2
  199.8 1.1 copy.68
  200.9 3.4 %collective-permute-done.2 = bf16[8,4096]{1,0:T(8,128)(2,1)S(1)} collective-permute-done((bf16[8,4096]{1,0:T(8,128)(2,1)S(1)}, bf16[8,4096]{1,0:T(8,128)(2,1)S(1)}, u32[]{:S(2)}, u32[]{:S(2)}) %collective-permute-start.2) | collective-permute-done | bytes 65568 | tf_op jit(solution)/shard_map/ppermute | solution.py:245
  204.4 1.1 copy.69
  (45 shorter events, 9.5 us)
Async XLA Ops:
  7.2 70.0 %all-gather.3.cloned.1.call-start = ((), (), s32[]{:S(2)}) async-start(), calls=%async_computation.2 | async-start | bytes 8912896 | tf_op jit(solution)/shard_map/all_gather | solution.py:189
  13.4 5.2 %copy-start.3 = (bf16[1,1,2,256,128]{4,3,2,1,0:T(8,128)(2,1)S(1)}, bf16[1,1,2,256,128]{4,3,2,1,0:T(8,128)(2,1)}, u32[]{:S(2)}) copy-start(bf16[1,1,2,256,128]{4,3,2,1,0:T(8,128)(2,1)} %param.10) | copy-start | bytes 393220
  14.5 6.1 %copy-start.4 = (s32[1,1,16]{2,1,0:T(1,128)S(1)}, s32[1,1,16]{2,1,0:T(1,128)}, u32[]{:S(2)}) copy-start(s32[1,1,16]{2,1,0:T(1,128)} %param.12) | copy-start | bytes 196
  18.4 167.0 %reduce-scatter.2.cloned.1.call-start = ((), (), s32[]{:S(2)}) async-start(), calls=%async_computation.1 | async-start | bytes 4456448 | tf_op jit(solution)/shard_map/reduce_scatter | solution.py:222
  18.9 58.2 %copy-start = (bf16[2,256,16,2,8]{1,4,0,3,2:T(8,128)(2,1)}, bf16[2,256,16,2,8]{1,4,0,3,2:T(8,128)(2,1)S(1)}, u32[]{:S(2)}) copy-start(bf16[2,256,16,2,8]{1,4,0,3,2:T(8,128)(2,1)S(1)} %copy.48) | copy-start | bytes 786436
  117.3 1.0 copy-start.1
  118.7 15.7 %collective-permute-start = (bf16[3,4,4096]{2,0,1:T(4,128)(2,1)S(1)}, bf16[3,4,4096]{2,0,1:T(4,128)(2,1)S(1)}, u32[]{:S(2)}, u32[]{:S(2)}) collective-permute-start(bf16[3,4,4096]{2,0,1:T(4,128)(2,1)S(1)} %slice.137), channel_id=1, source_target_pairs={{0,2},{2,4},{4,6},{6,8},{8,10},{10,12},{12,14},{14,16},{16,18},{18... | collective-permute-start | bytes 294920 | tf_op jit(solution)/shard_map/ppermute | solution.py:28
  187.0 17.3 %copy-start.2 = (f32[8,4096]{1,0:T(8,128)S(1)}, f32[8,4096]{1,0:T(8,128)}, u32[]{:S(2)}) copy-start(f32[8,4096]{1,0:T(8,128)} %param.9) | copy-start | bytes 393220
  189.7 7.0 %collective-permute-start.1 = (bf16[3,4,4096]{2,0,1:T(4,128)(2,1)S(1)}, bf16[3,4,4096]{2,0,1:T(4,128)(2,1)S(1)}, u32[]{:S(2)}, u32[]{:S(2)}) collective-permute-start(bf16[3,4,4096]{2,0,1:T(4,128)(2,1)S(1)} %slice.136), channel_id=1, source_target_pairs={{2,0},{4,2},{6,4},{8,6},{10,8},{12,10},{14,12},{16,14},{18,16},{20... | collective-permute-start | bytes 294920 | tf_op jit(solution)/shard_map/ppermute | solution.py:28
  198.4 5.9 %collective-permute-start.2 = (bf16[8,4096]{1,0:T(8,128)(2,1)S(1)}, bf16[8,4096]{1,0:T(8,128)(2,1)S(1)}, u32[]{:S(2)}, u32[]{:S(2)}) collective-permute-start(bf16[8,4096]{1,0:T(8,128)(2,1)S(1)} %convert_element_type.171), channel_id=1, source_target_pairs={{0,1},{1,0},{2,3},{3,2},{4,5},{5,4},{6,7},{7,6},{8,9},{9,8},{10,11... | collective-permute-start | bytes 196616 | tf_op jit(solution)/shard_map/ppermute | solution.py:245
Sparse Core Ops, SparseCore 0:
  18.5 58.6 all-gather.2
  117.4 67.8 reduce-scatter.1
